TPU v7x, 32 devices: a whole 2x2x4 slice. The times are simulated.
32 devices in a mesh: dp: 8 (over y, x, core), ctx: 4 (over z).
Axes of the slice: x: 2, y: 2, z: 4, core: 2. Of those that a mesh axis runs over, the one named last changes fastest.
Arguments:
- inputs: bfloat16 [16, 1024, 768], P('dp', 'ctx'), may hold values from -6 to 6
- lengths: int32 [16], P('dp'), may hold values from 921 to 1024, as said below
- ln1_gain: bfloat16 [768], P(('dp', 'ctx')), may hold values from 0.5 to 1.5
- ln1_bias: bfloat16 [768], P(('dp', 'ctx')), may hold values from -4 to 4
- query_weight: bfloat16 [768, 768], P(('dp', 'ctx')), may hold values from -0.3125 to 0.3125
- query_bias: bfloat16 [768], P(('dp', 'ctx')), may hold values from -4 to 4
- key_weight: bfloat16 [768, 768], P(('dp', 'ctx')), may hold values from -0.3125 to 0.3125
- value_weight: bfloat16 [768, 768], P(('dp', 'ctx')), may hold values from -0.21875 to 0.21875
- value_bias: bfloat16 [768], P(('dp', 'ctx')), may hold values from -0.75 to 0.75
- out_weight: bfloat16 [768, 768], P(('dp', 'ctx')), may hold values from -1.75 to 1.75
- out_bias: bfloat16 [768], P(('dp', 'ctx')), may hold values from -4 to 4
- ln2_gain: bfloat16 [768], P(('dp', 'ctx')), may hold values from 0.5 to 1.5
- ln2_bias: bfloat16 [768], P(('dp', 'ctx')), may hold values from -4 to 4
- ffn_in_weight: bfloat16 [768, 3072], P(('dp', 'ctx')), may hold values from -0.21875 to 0.21875
- ffn_in_bias: bfloat16 [3072], P(('dp', 'ctx')), may hold values from -4 to 4
- ffn_out_weight: bfloat16 [3072, 768], P(('dp', 'ctx')), may hold values from -0.15625 to 0.15625
- ffn_out_bias: bfloat16 [768], P(('dp', 'ctx')), may hold values from -4 to 4
- out_grad: bfloat16 [16, 1024, 768], P('dp', 'ctx'), may hold values from -6 to 6
Outputs:
- output: bfloat16 [16, 1024, 768], P('dp', 'ctx')
- input_grad: bfloat16 [16, 1024, 768], P('dp', 'ctx')
- grad_ln1_gain: float32 [768], P(('dp', 'ctx'))
- grad_ln1_bias: float32 [768], P(('dp', 'ctx'))
- grad_query: float32 [768, 768], P(('dp', 'ctx'))
- grad_query_bias: float32 [768], P(('dp', 'ctx'))
- grad_key: float32 [768, 768], P(('dp', 'ctx'))
- grad_value: float32 [768, 768], P(('dp', 'ctx'))
- grad_value_bias: float32 [768], P(('dp', 'ctx'))
- grad_out: float32 [768, 768], P(('dp', 'ctx'))
- grad_out_bias: float32 [768], P(('dp', 'ctx'))
- grad_ln2_gain: float32 [768], P(('dp', 'ctx'))
- grad_ln2_bias: float32 [768], P(('dp', 'ctx'))
- grad_ffn_in: float32 [768, 3072], P(('dp', 'ctx'))
- grad_ffn_in_bias: float32 [3072], P(('dp', 'ctx'))
- grad_ffn_out: float32 [3072, 768], P(('dp', 'ctx'))
- grad_ffn_out_bias: float32 [768], P(('dp', 'ctx'))
Inputs may be any that keep to these rules, and one draw needn't show every extreme that they name: `lengths`: A sequence's molecules occupy positions 0 to its length - 1; some sequence has exactly 1024, some exactly 921.
All inputs are finite; a program needn't handle non-finite values.
Results may differ from a plain program's by a relative error of at most 0.015.
Values may be sent and summed in bfloat16 or wider, within the bound.
No kernel may reach another device: no remote copies, remote signals or barrier semaphores. Data moves between devices by JAX's collectives and lax.ppermute only.
A program may use at most 192 MiB of HBM per device.

v0:
```python
import jax
import jax.numpy as jnp
from jax import lax
from jax.sharding import PartitionSpec as P

H = 12
HD = 64


def layer_norm(tok_rows, gain, shift):
    center = tok_rows - jnp.mean(tok_rows, axis=-1, keepdims=True)
    spread = jnp.mean(center * center, axis=-1, keepdims=True)
    return center * lax.rsqrt(spread + 1e-06) * gain + shift


def gelu_exact(values):
    return jax.nn.gelu(values, approximate=False)


def outer_product(left_rows, right_rows):
    return lax.dot_general(
        left_rows, right_rows, (((0,), (0,)), ((), ())), preferred_element_type=jnp.float32
    )


def back_product(grad_rows, weight):
    return lax.dot_general(
        grad_rows, weight, (((1,), (1,)), ((), ())), preferred_element_type=jnp.float32
    )


def column_sum(grad_rows):
    return jnp.sum(grad_rows.astype(jnp.float32), axis=0)


def fetch(shards):
    return (
        lax.all_gather(shards[0], ("dp", "ctx"), axis=0, tiled=True),
        lax.all_gather(shards[1], ("dp", "ctx"), axis=0, tiled=True),
        lax.all_gather(shards[2], ("dp", "ctx"), axis=0, tiled=True),
        lax.all_gather(shards[3], ("dp", "ctx"), axis=0, tiled=True),
        lax.all_gather(shards[4], ("dp", "ctx"), axis=0, tiled=True),
        lax.all_gather(shards[5], ("dp", "ctx"), axis=0, tiled=True),
        lax.all_gather(shards[6], ("dp", "ctx"), axis=0, tiled=True),
        lax.all_gather(shards[7], ("dp", "ctx"), axis=0, tiled=True),
        lax.all_gather(shards[8], ("dp", "ctx"), axis=0, tiled=True),
        lax.all_gather(shards[9], ("dp", "ctx"), axis=0, tiled=True),
        lax.all_gather(shards[10], ("dp", "ctx"), axis=0, tiled=True),
        lax.all_gather(shards[11], ("dp", "ctx"), axis=0, tiled=True),
        lax.all_gather(shards[12], ("dp", "ctx"), axis=0, tiled=True),
        lax.all_gather(shards[13], ("dp", "ctx"), axis=0, tiled=True),
        lax.all_gather(shards[14], ("dp", "ctx"), axis=0, tiled=True),
    )


def forward(tok_block, length, full_set):
    (
        ln1_gain,
        ln1_bias,
        query_weight,
        query_bias,
        key_weight,
        value_weight,
        value_bias,
        out_weight,
        out_bias,
        ln2_gain,
        ln2_bias,
        ffn_in_weight,
        ffn_in_bias,
        ffn_out_weight,
        ffn_out_bias,
    ) = full_set
    seq_rows = tok_block.shape[0]
    tok_rows = tok_block.astype(jnp.float32)
    normed = layer_norm(
        tok_rows, ln1_gain.astype(jnp.float32), ln1_bias.astype(jnp.float32)
    ).astype(jnp.bfloat16)
    queries = (
        jnp.dot(normed, query_weight, preferred_element_type=jnp.float32)
        + query_bias.astype(jnp.float32)
    ).astype(jnp.bfloat16)
    key_rows = jnp.dot(normed, key_weight, preferred_element_type=jnp.float32).astype(jnp.bfloat16)
    value_rows = (
        jnp.dot(normed, value_weight, preferred_element_type=jnp.float32)
        + value_bias.astype(jnp.float32)
    ).astype(jnp.bfloat16)
    all_keys, all_values = (
        lax.all_gather(key_rows, "ctx", axis=0, tiled=True),
        lax.all_gather(value_rows, "ctx", axis=0, tiled=True),
    )
    total_rows = all_keys.shape[0]
    query_heads = queries.reshape(seq_rows, H, HD)
    key_heads = all_keys.reshape(total_rows, H, HD)
    value_heads = all_values.reshape(total_rows, H, HD)
    scores = jnp.einsum(
        "qhd,khd->hqk", query_heads, key_heads, preferred_element_type=jnp.float32
    ) * HD ** (-0.5)
    valid = jnp.arange(total_rows) < length
    scores = jnp.where(valid[None, None, :], scores, -1e30)
    log_total = jax.nn.logsumexp(scores, axis=-1)
    attn_probs = jax.nn.softmax(scores, axis=-1)
    low_probs = attn_probs.astype(jnp.bfloat16)
    mixed_rows = jnp.einsum(
        "hqk,khd->qhd", low_probs, value_heads, preferred_element_type=jnp.float32
    )
    mixed_rows = mixed_rows.reshape(seq_rows, H * HD).astype(jnp.bfloat16)
    middle = (
        tok_rows
        + jnp.dot(mixed_rows, out_weight, preferred_element_type=jnp.float32)
        + out_bias.astype(jnp.float32)
    )
    normed_two = layer_norm(
        middle, ln2_gain.astype(jnp.float32), ln2_bias.astype(jnp.float32)
    ).astype(jnp.bfloat16)
    ffn_pre = jnp.dot(
        normed_two, ffn_in_weight, preferred_element_type=jnp.float32
    ) + ffn_in_bias.astype(jnp.float32)
    ffn_act = gelu_exact(ffn_pre).astype(jnp.bfloat16)
    result = (
        middle
        + jnp.dot(ffn_act, ffn_out_weight, preferred_element_type=jnp.float32)
        + ffn_out_bias.astype(jnp.float32)
    )
    kept = (
        tok_rows,
        normed,
        query_heads,
        key_heads,
        value_heads,
        attn_probs,
        low_probs,
        mixed_rows,
        middle,
        normed_two,
        ffn_pre,
        ffn_act,
        log_total,
        length,
    )
    return (result.astype(jnp.bfloat16), kept)


def backward(kept, cot_block, full_set):
    (
        ln1_gain,
        ln1_bias,
        query_weight,
        query_bias,
        key_weight,
        value_weight,
        value_bias,
        out_weight,
        out_bias,
        ln2_gain,
        ln2_bias,
        ffn_in_weight,
        ffn_in_bias,
        ffn_out_weight,
        ffn_out_bias,
    ) = full_set
    (
        tok_rows,
        normed,
        query_heads,
        key_heads,
        value_heads,
        attn_probs,
        low_probs,
        mixed_rows,
        middle,
        normed_two,
        ffn_pre,
        ffn_act,
        log_total,
        length,
    ) = kept
    seq_rows = tok_rows.shape[0]
    total_rows = key_heads.shape[0]
    score_scale = HD ** (-0.5)
    d_out = cot_block.astype(jnp.float32)
    d_ffn_out = d_out.astype(jnp.bfloat16)
    grad_ffn_out_bias = column_sum(d_ffn_out)
    grad_ffn_out = outer_product(ffn_act, d_ffn_out)
    d_act = back_product(d_ffn_out, ffn_out_weight)
    unused, gelu_back = jax.vjp(gelu_exact, ffn_pre)
    d_pre = gelu_back(d_act)[0].astype(jnp.bfloat16)
    grad_ffn_in_bias = column_sum(d_pre)
    grad_ffn_in = outer_product(normed_two, d_pre)
    d_normed_two = back_product(d_pre, ffn_in_weight)
    unused, second_back = jax.vjp(
        layer_norm, middle, ln2_gain.astype(jnp.float32), ln2_bias.astype(jnp.float32)
    )
    d_middle, grad_ln2_gain, grad_ln2_bias = second_back(d_normed_two)
    d_middle = d_middle + d_out
    d_branch = d_middle.astype(jnp.bfloat16)
    grad_out_bias = column_sum(d_branch)
    grad_out = outer_product(mixed_rows, d_branch)
    d_mixed = back_product(d_branch, out_weight).astype(jnp.bfloat16).reshape(seq_rows, H, HD)
    d_probs = jnp.einsum("qhd,khd->hqk", d_mixed, value_heads, preferred_element_type=jnp.float32)
    row_inner = jnp.sum(attn_probs * d_probs, axis=-1, keepdims=True)
    d_scores = (attn_probs * (d_probs - row_inner)).astype(jnp.bfloat16)
    d_query = (
        jnp.einsum("hqk,khd->qhd", d_scores, key_heads, preferred_element_type=jnp.float32)
        * score_scale
    )
    d_query = d_query.reshape(seq_rows, H * HD).astype(jnp.bfloat16)
    key_terms = (
        jnp.einsum("hqk,qhd->khd", d_scores, query_heads, preferred_element_type=jnp.float32)
        * score_scale
    )
    value_terms = jnp.einsum("hqk,qhd->khd", low_probs, d_mixed, preferred_element_type=jnp.float32)
    key_sums, value_sums = (
        lax.psum_scatter(
            key_terms.reshape(total_rows, H * HD).astype(jnp.bfloat16),
            "ctx",
            scatter_dimension=0,
            tiled=True,
        ).astype(jnp.float32),
        lax.psum_scatter(
            value_terms.reshape(total_rows, H * HD).astype(jnp.bfloat16),
            "ctx",
            scatter_dimension=0,
            tiled=True,
        ).astype(jnp.float32),
    )
    d_key = key_sums.astype(jnp.bfloat16)
    d_value = value_sums.astype(jnp.bfloat16)
    grad_query_bias = column_sum(d_query)
    grad_value_bias = column_sum(d_value)
    grad_query = outer_product(normed, d_query)
    grad_key = outer_product(normed, d_key)
    grad_value = outer_product(normed, d_value)
    d_normed = (
        back_product(d_query, query_weight)
        + back_product(d_key, key_weight)
        + back_product(d_value, value_weight)
    )
    unused, first_back = jax.vjp(
        layer_norm, tok_rows, ln1_gain.astype(jnp.float32), ln1_bias.astype(jnp.float32)
    )
    d_rows, grad_ln1_gain, grad_ln1_bias = first_back(d_normed)
    d_input = (d_middle + d_rows).astype(jnp.bfloat16)
    grads = (
        grad_ln1_gain,
        grad_ln1_bias,
        grad_query,
        grad_query_bias,
        grad_key,
        grad_value,
        grad_value_bias,
        grad_out,
        grad_out_bias,
        grad_ln2_gain,
        grad_ln2_bias,
        grad_ffn_in,
        grad_ffn_in_bias,
        grad_ffn_out,
        grad_ffn_out_bias,
    )
    return (d_input, grads)


def per_device(
    inputs,
    lengths,
    ln1_gain,
    ln1_bias,
    query_weight,
    query_bias,
    key_weight,
    value_weight,
    value_bias,
    out_weight,
    out_bias,
    ln2_gain,
    ln2_bias,
    ffn_in_weight,
    ffn_in_bias,
    ffn_out_weight,
    ffn_out_bias,
    out_grad,
):
    shards = (
        ln1_gain,
        ln1_bias,
        query_weight,
        query_bias,
        key_weight,
        value_weight,
        value_bias,
        out_weight,
        out_bias,
        ln2_gain,
        ln2_bias,
        ffn_in_weight,
        ffn_in_bias,
        ffn_out_weight,
        ffn_out_bias,
    )

    def forward_step(counter, seq_entry):
        tok_block, length = seq_entry
        result, kept = forward(tok_block, length, fetch(shards))
        return (counter, result)

    counter, output = lax.scan(forward_step, jnp.zeros((), jnp.int32), (inputs, lengths))

    def backward_step(totals, seq_entry):
        tok_block, length, cot_block = seq_entry
        full_set = fetch(shards)
        unused, kept = forward(tok_block, length, full_set)
        d_input, grads = backward(kept, cot_block, full_set)
        return (jax.tree.map(jnp.add, totals, grads), d_input)

    groups = lax.axis_size(("dp", "ctx"))
    start_totals = tuple(
        (
            jnp.zeros((shard_item.shape[0] * groups,) + shard_item.shape[1:], jnp.float32)
            for shard_item in shards
        )
    )
    totals, input_grad = lax.scan(backward_step, start_totals, (inputs, lengths, out_grad))
    grad_shards = lax.psum_scatter(totals, ("dp", "ctx"), scatter_dimension=0, tiled=True)
    return (output, input_grad) + tuple(grad_shards)


def solution(mesh):
    return jax.shard_map(
        per_device,
        mesh=mesh,
        in_specs=(
            P("dp", "ctx", None),
            P("dp"),
            P(("dp", "ctx")),
            P(("dp", "ctx")),
            P(("dp", "ctx"), None),
            P(("dp", "ctx")),
            P(("dp", "ctx"), None),
            P(("dp", "ctx"), None),
            P(("dp", "ctx")),
            P(("dp", "ctx"), None),
            P(("dp", "ctx")),
            P(("dp", "ctx")),
            P(("dp", "ctx")),
            P(("dp", "ctx"), None),
            P(("dp", "ctx")),
            P(("dp", "ctx"), None),
            P(("dp", "ctx")),
            P("dp", "ctx", None),
        ),
        out_specs=(
            P("dp", "ctx", None),
            P("dp", "ctx", None),
            P(("dp", "ctx")),
            P(("dp", "ctx")),
            P(("dp", "ctx"), None),
            P(("dp", "ctx")),
            P(("dp", "ctx"), None),
            P(("dp", "ctx"), None),
            P(("dp", "ctx")),
            P(("dp", "ctx"), None),
            P(("dp", "ctx")),
            P(("dp", "ctx")),
            P(("dp", "ctx")),
            P(("dp", "ctx"), None),
            P(("dp", "ctx")),
            P(("dp", "ctx"), None),
            P(("dp", "ctx")),
        ),
        check_vma=False,
    )
```

profile of v0, /device:TPU:0, one launch (start us, length us, event | category | flops | bytes accessed | tf_op | source)
XLA Modules:
  0.0 2723.2 jit_solution(3749500177245971645)
XLA Ops:
  8.2 888.4 %while.51 = (s32[]{:T(128)}, bf16[2,256,768]{2,1,0:T(8,128)(2,1)S(1)}, bf16[2,256,768]{2,1,0:T(8,128)(2,1)}, bf16[24]{0:T(256)(128)(2,1)}, bf16[24]{0:T(256)(128...) while((s32[]{:T(128)}, ...), condition=%wide.region_7.8_spmd, body=%wide.region_0.7_spmd.sunk | while | flops 4508832256 | bytes 116793320 | solution.py:307
  18.1 42.5 %all-reduce.39 = (bf16[768]{0:T(1024)(128)(2,1)S(1)}, bf16[768]{0:T(1024)(128)(2,1)S(1)}, bf16[768]{0:T(1024)(128)(2,1)S(1)}, bf16[768]{0:T(1024)(128)(2,1)S(1)}...) all-reduce(bf16[768]{0:T(1024)(128)(2,1)S(1)} %dynamic-update-slice, ...), channel_id=1, replica_groups=mesh['dp'=8,'ctx'=4] {'dp','ctx'}, use_global_device_ids=true, to_apply=%add.2 | all-reduce | flops 9216 | bytes 36864 | tf_op jit(solution)/shard_map/while
  71.7 52.9 %all-gather.17.cloned.1.call-done = bf16[768,768]{1,0:T(8,128)(2,1)} async-done(((bf16[24,768]{1,0:T(8,128)(2,1)}), bf16[768,768]{1,0:T(8,128)(2,1)}) %all-gather.17.cloned.1.call-update) | async-done | bytes 1179664 | tf_op jit(solution)/shard_map/while/body/eval_jaxpr/all_gather | solution.py:43
  132.9 47.5 %all-gather.21.cloned.1.call-done = bf16[768,768]{1,0:T(8,128)(2,1)} async-done(((bf16[24,768]{1,0:T(8,128)(2,1)}), bf16[768,768]{1,0:T(8,128)(2,1)}) %all-gather.21.cloned.1.call-update) | async-done | bytes 1179664 | tf_op jit(solution)/shard_map/while/body/eval_jaxpr/all_gather | solution.py:40
  182.3 36.0 %all-gather.25.cloned.1.call-done = bf16[1024,768]{1,0:T(8,128)(2,1)} async-done(((bf16[256,768]{1,0:T(8,128)(2,1)}), bf16[1024,768]{1,0:T(8,128)(2,1)}) %all-gather.25.cloned.1.call-update) | async-done | bytes 1572880 | tf_op jit(solution)/shard_map/while/body/eval_jaxpr/all_gather | solution.py:89
  220.0 36.2 %all-gather.19.cloned.1.call-done = bf16[1024,768]{1,0:T(8,128)(2,1)} async-done(((bf16[256,768]{1,0:T(8,128)(2,1)}), bf16[1024,768]{1,0:T(8,128)(2,1)}) %all-gather.19.cloned.1.call-update) | async-done | bytes 1572880 | tf_op jit(solution)/shard_map/while/body/eval_jaxpr/all_gather | solution.py:90
  258.9 8.2 fusion.313
  267.1 7.1 fusion.314
  274.2 37.6 %all-gather.27.cloned.1.call-done = bf16[768,768]{1,0:T(8,128)(2,1)} async-done(((bf16[24,768]{1,0:T(8,128)(2,1)}), bf16[768,768]{1,0:T(8,128)(2,1)}) %all-gather.27.cloned.1.call-update) | async-done | bytes 1179664 | tf_op jit(solution)/shard_map/while/body/eval_jaxpr/all_gather | solution.py:45
  313.9 63.2 %all-gather.29.cloned.1.call-done = bf16[3072,768]{1,0:T(8,128)(2,1)} async-done(((bf16[96,768]{1,0:T(8,128)(2,1)}), bf16[3072,768]{1,0:T(8,128)(2,1)}) %all-gather.29.cloned.1.call-update) | async-done | bytes 4718608 | tf_op jit(solution)/shard_map/while/body/eval_jaxpr/all_gather | solution.py:51
  377.1 64.7 %all-gather.31.cloned.1.call-done = bf16[768,3072]{1,0:T(8,128)(2,1)} async-done(((bf16[24,3072]{1,0:T(8,128)(2,1)}), bf16[768,3072]{1,0:T(8,128)(2,1)}) %all-gather.31.cloned.1.call-update) | async-done | bytes 4718608 | tf_op jit(solution)/shard_map/while/body/eval_jaxpr/all_gather | solution.py:49
  441.9 12.9 fusion.316
  464.4 39.8 %all-reduce.39 = (bf16[768]{0:T(1024)(128)(2,1)S(1)}, bf16[768]{0:T(1024)(128)(2,1)S(1)}, bf16[768]{0:T(1024)(128)(2,1)S(1)}, bf16[768]{0:T(1024)(128)(2,1)S(1)}...) all-reduce(bf16[768]{0:T(1024)(128)(2,1)S(1)} %dynamic-update-slice, ...), channel_id=1, replica_groups=mesh['dp'=8,'ctx'=4] {'dp','ctx'}, use_global_device_ids=true, to_apply=%add.2 | all-reduce | flops 9216 | bytes 36864 | tf_op jit(solution)/shard_map/while
  513.7 52.9 %all-gather.17.cloned.1.call-done = bf16[768,768]{1,0:T(8,128)(2,1)} async-done(((bf16[24,768]{1,0:T(8,128)(2,1)}), bf16[768,768]{1,0:T(8,128)(2,1)}) %all-gather.17.cloned.1.call-update) | async-done | bytes 1179664 | tf_op jit(solution)/shard_map/while/body/eval_jaxpr/all_gather | solution.py:43
  574.6 47.8 %all-gather.21.cloned.1.call-done = bf16[768,768]{1,0:T(8,128)(2,1)} async-done(((bf16[24,768]{1,0:T(8,128)(2,1)}), bf16[768,768]{1,0:T(8,128)(2,1)}) %all-gather.21.cloned.1.call-update) | async-done | bytes 1179664 | tf_op jit(solution)/shard_map/while/body/eval_jaxpr/all_gather | solution.py:40
  624.4 36.0 %all-gather.25.cloned.1.call-done = bf16[1024,768]{1,0:T(8,128)(2,1)} async-done(((bf16[256,768]{1,0:T(8,128)(2,1)}), bf16[1024,768]{1,0:T(8,128)(2,1)}) %all-gather.25.cloned.1.call-update) | async-done | bytes 1572880 | tf_op jit(solution)/shard_map/while/body/eval_jaxpr/all_gather | solution.py:89
  662.1 36.3 %all-gather.19.cloned.1.call-done = bf16[1024,768]{1,0:T(8,128)(2,1)} async-done(((bf16[256,768]{1,0:T(8,128)(2,1)}), bf16[1024,768]{1,0:T(8,128)(2,1)}) %all-gather.19.cloned.1.call-update) | async-done | bytes 1572880 | tf_op jit(solution)/shard_map/while/body/eval_jaxpr/all_gather | solution.py:90
  701.1 8.2 fusion.313
  709.3 7.1 fusion.314
  716.4 37.6 %all-gather.27.cloned.1.call-done = bf16[768,768]{1,0:T(8,128)(2,1)} async-done(((bf16[24,768]{1,0:T(8,128)(2,1)}), bf16[768,768]{1,0:T(8,128)(2,1)}) %all-gather.27.cloned.1.call-update) | async-done | bytes 1179664 | tf_op jit(solution)/shard_map/while/body/eval_jaxpr/all_gather | solution.py:45
  756.1 63.1 %all-gather.29.cloned.1.call-done = bf16[3072,768]{1,0:T(8,128)(2,1)} async-done(((bf16[96,768]{1,0:T(8,128)(2,1)}), bf16[3072,768]{1,0:T(8,128)(2,1)}) %all-gather.29.cloned.1.call-update) | async-done | bytes 4718608 | tf_op jit(solution)/shard_map/while/body/eval_jaxpr/all_gather | solution.py:51
  819.2 64.6 %all-gather.31.cloned.1.call-done = bf16[768,3072]{1,0:T(8,128)(2,1)} async-done(((bf16[24,3072]{1,0:T(8,128)(2,1)}), bf16[768,3072]{1,0:T(8,128)(2,1)}) %all-gather.31.cloned.1.call-update) | async-done | bytes 4718608 | tf_op jit(solution)/shard_map/while/body/eval_jaxpr/all_gather | solution.py:49
  883.8 12.9 fusion.316
  897.8 1116.4 %while.52 = (s32[]{:T(128)}, f32[768]{0:T(1024)}, f32[768]{0:T(1024)}, f32[768,768]{1,0:T(8,128)}, f32[768]{0:T(1024)}, /*index=5*/f32[768,768]{1,0:T(8,128)}, f...) while((s32[]{:T(128)}, f32[768]{0:T(1024)}, ...), condition=%wide.region_31.32_spmd.clone, body=%wide.region_8.31_spmd.clone.sunk | while | flops 12278196224 | bytes 516163296 | solution.py:323
  930.1 39.5 %all-reduce.40 = (bf16[768]{0:T(1024)(128)(2,1)S(1)}, bf16[768]{0:T(1024)(128)(2,1)S(1)}, bf16[3072]{0:T(1024)(128)(2,1)S(1)}, bf16[768]{0:T(1024)(128)(2,1)S(1)...) all-reduce(bf16[768]{0:T(1024)(128)(2,1)S(1)} %dynamic-update-slice, ...), channel_id=1, replica_groups=mesh['dp'=8,'ctx'=4] {'dp','ctx'}, use_global_device_ids=true, to_apply=%add.10 | all-reduce | flops 8448 | bytes 33792 | tf_op jit(solution)/shard_map/while
  980.1 52.9 %all-gather.33.cloned.1.call-done = bf16[768,768]{1,0:T(8,128)(2,1)} async-done(((bf16[24,768]{1,0:T(8,128)(2,1)}), bf16[768,768]{1,0:T(8,128)(2,1)}) %all-gather.33.cloned.1.call-update) | async-done | bytes 1179664 | tf_op jit(solution)/shard_map/while/body/eval_jaxpr/all_gather | solution.py:42
  1039.0 49.7 %all-gather.37.cloned.1.call-done = bf16[768,768]{1,0:T(8,128)(2,1)} async-done(((bf16[24,768]{1,0:T(8,128)(2,1)}), bf16[768,768]{1,0:T(8,128)(2,1)}) %all-gather.37.cloned.1.call-update) | async-done | bytes 1179664 | tf_op jit(solution)/shard_map/while/body/eval_jaxpr/all_gather | solution.py:40
  1090.7 35.4 %all-gather.41.cloned.1.call-done = bf16[1024,768]{1,0:T(8,128)(2,1)} async-done(((bf16[256,768]{1,0:T(8,128)(2,1)}), bf16[1024,768]{1,0:T(8,128)(2,1)}) %all-gather.41.cloned.1.call-update) | async-done | bytes 1572880 | tf_op jit(solution)/shard_map/while/body/eval_jaxpr/all_gather | solution.py:90
  1128.7 34.9 %all-gather.35.cloned.1.call-done = bf16[1024,768]{1,0:T(8,128)(2,1)} async-done(((bf16[256,768]{1,0:T(8,128)(2,1)}), bf16[1024,768]{1,0:T(8,128)(2,1)}) %all-gather.35.cloned.1.call-update) | async-done | bytes 1572880 | tf_op jit(solution)/shard_map/while/body/eval_jaxpr/all_gather | solution.py:89
  1165.3 7.0 fusion.362
  1172.3 7.2 fusion.364
  1179.5 39.8 %all-gather.43.cloned.1.call-done = bf16[768,768]{1,0:T(8,128)(2,1)} async-done(((bf16[24,768]{1,0:T(8,128)(2,1)}), bf16[768,768]{1,0:T(8,128)(2,1)}) %all-gather.43.cloned.1.call-update) | async-done | bytes 1179664 | tf_op jit(solution)/shard_map/while/body/eval_jaxpr/all_gather | solution.py:45
  1221.4 63.2 %all-gather.45.cloned.1.call-done = bf16[768,3072]{1,0:T(8,128)(2,1)} async-done(((bf16[24,3072]{1,0:T(8,128)(2,1)}), bf16[768,3072]{1,0:T(8,128)(2,1)}) %all-gather.45.cloned.1.call-update) | async-done | bytes 4718608 | tf_op jit(solution)/shard_map/while/body/eval_jaxpr/all_gather | solution.py:49
  1290.1 59.1 %all-gather.47.cloned.1.call-done = bf16[3072,768]{1,0:T(8,128)(2,1)} async-done(((bf16[96,768]{1,0:T(8,128)(2,1)}), bf16[3072,768]{1,0:T(8,128)(2,1)}) %all-gather.47.cloned.1.call-update) | async-done | bytes 4718608 | tf_op jit(solution)/shard_map/while/body/eval_jaxpr/all_gather | solution.py:51
  1349.2 11.1 convert_reduce_fusion.15
  1366.9 10.9 multiply_reduce_fusion.12
  1397.8 6.6 select_add_fusion.36
  1404.5 7.4 fusion.369
  1418.9 10.0 select_add_fusion.38
  1431.0 28.6 %reduce-scatter.23.cloned.1.call-done = bf16[256,768]{0,1:T(8,128)(2,1)} async-done(((bf16[1024,768]{0,1:T(8,128)(2,1)}), bf16[256,768]{0,1:T(8,128)(2,1)}) %reduce-scatter.23.cloned.1.call-update) | async-done | bytes 393232 | tf_op jit(solution)/shard_map/while/body/eval_jaxpr/reduce_scatter | solution.py:220
  1476.3 39.7 %all-reduce.40 = (bf16[768]{0:T(1024)(128)(2,1)S(1)}, bf16[768]{0:T(1024)(128)(2,1)S(1)}, bf16[3072]{0:T(1024)(128)(2,1)S(1)}, bf16[768]{0:T(1024)(128)(2,1)S(1)...) all-reduce(bf16[768]{0:T(1024)(128)(2,1)S(1)} %dynamic-update-slice, ...), channel_id=1, replica_groups=mesh['dp'=8,'ctx'=4] {'dp','ctx'}, use_global_device_ids=true, to_apply=%add.10 | all-reduce | flops 8448 | bytes 33792 | tf_op jit(solution)/shard_map/while
  1526.7 53.0 %all-gather.33.cloned.1.call-done = bf16[768,768]{1,0:T(8,128)(2,1)} async-done(((bf16[24,768]{1,0:T(8,128)(2,1)}), bf16[768,768]{1,0:T(8,128)(2,1)}) %all-gather.33.cloned.1.call-update) | async-done | bytes 1179664 | tf_op jit(solution)/shard_map/while/body/eval_jaxpr/all_gather | solution.py:42
  1585.7 49.7 %all-gather.37.cloned.1.call-done = bf16[768,768]{1,0:T(8,128)(2,1)} async-done(((bf16[24,768]{1,0:T(8,128)(2,1)}), bf16[768,768]{1,0:T(8,128)(2,1)}) %all-gather.37.cloned.1.call-update) | async-done | bytes 1179664 | tf_op jit(solution)/shard_map/while/body/eval_jaxpr/all_gather | solution.py:40
  1637.4 35.4 %all-gather.41.cloned.1.call-done = bf16[1024,768]{1,0:T(8,128)(2,1)} async-done(((bf16[256,768]{1,0:T(8,128)(2,1)}), bf16[1024,768]{1,0:T(8,128)(2,1)}) %all-gather.41.cloned.1.call-update) | async-done | bytes 1572880 | tf_op jit(solution)/shard_map/while/body/eval_jaxpr/all_gather | solution.py:90
  1675.4 34.9 %all-gather.35.cloned.1.call-done = bf16[1024,768]{1,0:T(8,128)(2,1)} async-done(((bf16[256,768]{1,0:T(8,128)(2,1)}), bf16[1024,768]{1,0:T(8,128)(2,1)}) %all-gather.35.cloned.1.call-update) | async-done | bytes 1572880 | tf_op jit(solution)/shard_map/while/body/eval_jaxpr/all_gather | solution.py:89
  1712.0 6.9 fusion.362
  1719.0 7.2 fusion.364
  1726.2 39.8 %all-gather.43.cloned.1.call-done = bf16[768,768]{1,0:T(8,128)(2,1)} async-done(((bf16[24,768]{1,0:T(8,128)(2,1)}), bf16[768,768]{1,0:T(8,128)(2,1)}) %all-gather.43.cloned.1.call-update) | async-done | bytes 1179664 | tf_op jit(solution)/shard_map/while/body/eval_jaxpr/all_gather | solution.py:45
  1768.1 63.1 %all-gather.45.cloned.1.call-done = bf16[768,3072]{1,0:T(8,128)(2,1)} async-done(((bf16[24,3072]{1,0:T(8,128)(2,1)}), bf16[768,3072]{1,0:T(8,128)(2,1)}) %all-gather.45.cloned.1.call-update) | async-done | bytes 4718608 | tf_op jit(solution)/shard_map/while/body/eval_jaxpr/all_gather | solution.py:49
  1836.7 59.3 %all-gather.47.cloned.1.call-done = bf16[3072,768]{1,0:T(8,128)(2,1)} async-done(((bf16[96,768]{1,0:T(8,128)(2,1)}), bf16[3072,768]{1,0:T(8,128)(2,1)}) %all-gather.47.cloned.1.call-update) | async-done | bytes 4718608 | tf_op jit(solution)/shard_map/while/body/eval_jaxpr/all_gather | solution.py:51
  1895.9 11.1 convert_reduce_fusion.15
  1913.6 10.9 multiply_reduce_fusion.12
  1935.9 6.0 convert_reduce_fusion.17
  1944.5 9.4 select_add_fusion.36
  1954.0 7.4 fusion.369
  1970.9 12.1 select_add_fusion.38
  1985.0 21.3 reduce-scatter.23.cloned.1.call-done
  2018.2 40.0 %all-reduce.36 = (f32[768]{0:T(1024)S(1)}, f32[768]{0:T(1024)S(1)}, f32[768]{0:T(1024)S(1)}, f32[768]{0:T(1024)S(1)}, f32[768]{0:T(1024)S(1)}, /*index=5*/f32[76...) all-reduce(f32[768]{0:T(1024)S(1)} %copy-done.57, ...), channel_id=4, replica_groups=mesh['dp'=8,'ctx'=4] {'dp','ctx'}, use_global_device_ids=true, to_apply=%region_32.33.clone | all-reduce | flops 9216 | bytes 73728
  2063.5 55.5 %reduce-scatter.9.cloned.1.call-done = f32[24,768]{1,0:T(8,128)} async-done(((f32[768,768]{1,0:T(8,128)}), f32[24,768]{1,0:T(8,128)}) %reduce-scatter.9.cloned.1.call-update) | async-done | bytes 73744 | tf_op jit(solution)/shard_map/reduce_scatter | solution.py:324
  2119.1 104.4 %reduce-scatter.11.cloned.1.call-done = f32[24,768]{1,0:T(8,128)} async-done(((f32[768,768]{1,0:T(8,128)}), f32[24,768]{1,0:T(8,128)}) %reduce-scatter.11.cloned.1.call-update) | async-done | bytes 73744 | tf_op jit(solution)/shard_map/reduce_scatter | solution.py:324
  2223.5 104.3 %reduce-scatter.13.cloned.1.call-done = f32[24,768]{1,0:T(8,128)} async-done(((f32[768,768]{1,0:T(8,128)}), f32[24,768]{1,0:T(8,128)}) %reduce-scatter.13.cloned.1.call-update) | async-done | bytes 73744 | tf_op jit(solution)/shard_map/reduce_scatter | solution.py:324
  2327.8 104.5 %reduce-scatter.15.cloned.1.call-done = f32[24,768]{1,0:T(8,128)} async-done(((f32[768,768]{1,0:T(8,128)}), f32[24,768]{1,0:T(8,128)}) %reduce-scatter.15.cloned.1.call-update) | async-done | bytes 73744 | tf_op jit(solution)/shard_map/reduce_scatter | solution.py:324
  2432.3 141.7 %reduce-scatter.17.cloned.1.call-done = f32[24,3072]{1,0:T(8,128)} async-done(((f32[768,3072]{1,0:T(8,128)}), f32[24,3072]{1,0:T(8,128)}) %reduce-scatter.17.cloned.1.call-update) | async-done | bytes 294928 | tf_op jit(solution)/shard_map/reduce_scatter | solution.py:324
  2574.0 141.7 %reduce-scatter.19.cloned.1.call-done = f32[96,768]{1,0:T(8,128)} async-done(((f32[3072,768]{1,0:T(8,128)}), f32[96,768]{1,0:T(8,128)}) %reduce-scatter.19.cloned.1.call-update) | async-done | bytes 294928 | tf_op jit(solution)/shard_map/reduce_scatter | solution.py:324
  (607 shorter events, 243.8 us)
Async XLA Ops:
  8.2 116.4 %copy-start.1 = (bf16[2,256,768]{2,1,0:T(8,128)(2,1)S(1)}, bf16[2,256,768]{2,1,0:T(8,128)(2,1)}, u32[]{:S(2)}) copy-start(bf16[2,256,768]{2,1,0:T(8,128)(2,1)} %get-tuple-element.1061) | copy-start | bytes 2359300 | tf_op jit(solution)/shard_map/while
  8.2 60.6 %all-gather.23.cloned.1.call-start = ((), (), s32[]{:S(2)}) async-start(), calls=%async_computation.17 | async-start | bytes 1216512 | tf_op jit(solution)/shard_map/while/body/eval_jaxpr/all_gather | solution.py:42
  9.0 115.6 %all-gather.17.cloned.1.call-start = ((), (), s32[]{:S(2)}) async-start(), calls=%async_computation.14 | async-start | bytes 1216512 | tf_op jit(solution)/shard_map/while/body/eval_jaxpr/all_gather | solution.py:43
  9.7 170.6 %all-gather.21.cloned.1.call-start = ((), (), s32[]{:S(2)}) async-start(), calls=%async_computation.16 | async-start | bytes 1216512 | tf_op jit(solution)/shard_map/while/body/eval_jaxpr/all_gather | solution.py:40
  10.5 207.8 %all-gather.25.cloned.1.call-start = ((), (), s32[]{:S(2)}) async-start(), calls=%async_computation.18 | async-start | bytes 1966080 | tf_op jit(solution)/shard_map/while/body/eval_jaxpr/all_gather | solution.py:89
  63.0 66.3 %copy-start.64 = (s32[2]{0:T(128)S(1)}, s32[2]{0:T(128)}, u32[]{:S(2)}) copy-start(s32[2]{0:T(128)} %get-tuple-element.1066) | copy-start | bytes 28 | tf_op jit(solution)/shard_map/while
  71.6 184.6 %all-gather.19.cloned.1.call-start = ((), (), s32[]{:S(2)}) async-start(), calls=%async_computation.15 | async-start | bytes 1966080 | tf_op jit(solution)/shard_map/while/body/eval_jaxpr/all_gather | solution.py:90
  127.2 184.6 %all-gather.27.cloned.1.call-start = ((), (), s32[]{:S(2)}) async-start(), calls=%async_computation.19 | async-start | bytes 1216512 | tf_op jit(solution)/shard_map/while/body/eval_jaxpr/all_gather | solution.py:45
  127.8 249.4 %all-gather.29.cloned.1.call-start = ((), (), s32[]{:S(2)}) async-start(), calls=%async_computation.20 | async-start | bytes 4866048 | tf_op jit(solution)/shard_map/while/body/eval_jaxpr/all_gather | solution.py:51
  128.5 313.3 %all-gather.31.cloned.1.call-start = ((), (), s32[]{:S(2)}) async-start(), calls=%async_computation.21 | async-start | bytes 4866048 | tf_op jit(solution)/shard_map/while/body/eval_jaxpr/all_gather | solution.py:49
  274.2 167.7 %copy-start.60 = (f32[768]{0:T(1024)S(1)}, f32[768]{0:T(1024)}, u32[]{:S(2)}) copy-start(f32[768]{0:T(1024)} %convert_element_type.492) | copy-start | bytes 9220 | tf_op jit(solution)/shard_map/while
  274.2 167.7 %copy-start.61 = (f32[768]{0:T(1024)S(1)}, f32[768]{0:T(1024)}, u32[]{:S(2)}) copy-start(f32[768]{0:T(1024)} %convert_element_type.493) | copy-start | bytes 9220 | tf_op jit(solution)/shard_map/while
  274.2 167.7 %copy-start.62 = (f32[768]{0:T(1024)S(1)}, f32[768]{0:T(1024)}, u32[]{:S(2)}) copy-start(f32[768]{0:T(1024)} %convert_element_type.494) | copy-start | bytes 9220 | tf_op jit(solution)/shard_map/while
  454.7 111.9 %copy-start.1 = (bf16[2,256,768]{2,1,0:T(8,128)(2,1)S(1)}, bf16[2,256,768]{2,1,0:T(8,128)(2,1)}, u32[]{:S(2)}) copy-start(bf16[2,256,768]{2,1,0:T(8,128)(2,1)} %get-tuple-element.1061) | copy-start | bytes 2359300 | tf_op jit(solution)/shard_map/while
  454.8 56.2 %all-gather.23.cloned.1.call-start = ((), (), s32[]{:S(2)}) async-start(), calls=%async_computation.17 | async-start | bytes 1216512 | tf_op jit(solution)/shard_map/while/body/eval_jaxpr/all_gather | solution.py:42
  455.5 111.1 %all-gather.17.cloned.1.call-start = ((), (), s32[]{:S(2)}) async-start(), calls=%async_computation.14 | async-start | bytes 1216512 | tf_op jit(solution)/shard_map/while/body/eval_jaxpr/all_gather | solution.py:43
  456.1 166.3 %all-gather.21.cloned.1.call-start = ((), (), s32[]{:S(2)}) async-start(), calls=%async_computation.16 | async-start | bytes 1216512 | tf_op jit(solution)/shard_map/while/body/eval_jaxpr/all_gather | solution.py:40
  456.8 203.5 %all-gather.25.cloned.1.call-start = ((), (), s32[]{:S(2)}) async-start(), calls=%async_computation.18 | async-start | bytes 1966080 | tf_op jit(solution)/shard_map/while/body/eval_jaxpr/all_gather | solution.py:89
  513.7 184.7 %all-gather.19.cloned.1.call-start = ((), (), s32[]{:S(2)}) async-start(), calls=%async_computation.15 | async-start | bytes 1966080 | tf_op jit(solution)/shard_map/while/body/eval_jaxpr/all_gather | solution.py:90
  569.2 184.7 %all-gather.27.cloned.1.call-start = ((), (), s32[]{:S(2)}) async-start(), calls=%async_computation.19 | async-start | bytes 1216512 | tf_op jit(solution)/shard_map/while/body/eval_jaxpr/all_gather | solution.py:45
  569.8 249.4 %all-gather.29.cloned.1.call-start = ((), (), s32[]{:S(2)}) async-start(), calls=%async_computation.20 | async-start | bytes 4866048 | tf_op jit(solution)/shard_map/while/body/eval_jaxpr/all_gather | solution.py:51
  570.4 313.4 %all-gather.31.cloned.1.call-start = ((), (), s32[]{:S(2)}) async-start(), calls=%async_computation.21 | async-start | bytes 4866048 | tf_op jit(solution)/shard_map/while/body/eval_jaxpr/all_gather | solution.py:49
  716.4 167.4 %copy-start.60 = (f32[768]{0:T(1024)S(1)}, f32[768]{0:T(1024)}, u32[]{:S(2)}) copy-start(f32[768]{0:T(1024)} %convert_element_type.492) | copy-start | bytes 9220 | tf_op jit(solution)/shard_map/while
  716.4 167.4 %copy-start.61 = (f32[768]{0:T(1024)S(1)}, f32[768]{0:T(1024)}, u32[]{:S(2)}) copy-start(f32[768]{0:T(1024)} %convert_element_type.493) | copy-start | bytes 9220 | tf_op jit(solution)/shard_map/while
  716.4 167.4 %copy-start.62 = (f32[768]{0:T(1024)S(1)}, f32[768]{0:T(1024)}, u32[]{:S(2)}) copy-start(f32[768]{0:T(1024)} %convert_element_type.494) | copy-start | bytes 9220 | tf_op jit(solution)/shard_map/while
  921.3 111.6 %copy-start.2 = (bf16[2,256,768]{2,1,0:T(8,128)(2,1)S(1)}, bf16[2,256,768]{2,1,0:T(8,128)(2,1)}, u32[]{:S(2)}) copy-start(bf16[2,256,768]{2,1,0:T(8,128)(2,1)} %get-tuple-element.1180) | copy-start | bytes 2359300 | tf_op jit(solution)/shard_map/while
  921.4 56.0 %all-gather.39.cloned.1.call-start = ((), (), s32[]{:S(2)}) async-start(), calls=%async_computation.25 | async-start | bytes 1216512 | tf_op jit(solution)/shard_map/while/body/eval_jaxpr/all_gather | solution.py:43
  921.9 111.0 %all-gather.33.cloned.1.call-start = ((), (), s32[]{:S(2)}) async-start(), calls=%async_computation.22 | async-start | bytes 1216512 | tf_op jit(solution)/shard_map/while/body/eval_jaxpr/all_gather | solution.py:42
  922.5 166.2 %all-gather.37.cloned.1.call-start = ((), (), s32[]{:S(2)}) async-start(), calls=%async_computation.24 | async-start | bytes 1216512 | tf_op jit(solution)/shard_map/while/body/eval_jaxpr/all_gather | solution.py:40
  923.3 202.8 %all-gather.41.cloned.1.call-start = ((), (), s32[]{:S(2)}) async-start(), calls=%async_computation.26 | async-start | bytes 1966080 | tf_op jit(solution)/shard_map/while/body/eval_jaxpr/all_gather | solution.py:90
  970.7 118.0 %copy-start.20 = (f32[256]{0:T(256)}, f32[256]{0:T(256)S(1)}, u32[]{:S(2)}) copy-start(f32[256]{0:T(256)S(1)} %broadcast_multiply_fusion.10) | copy-start | bytes 3076 | tf_op jit(solution)/shard_map/while
  972.0 116.7 %copy-start.22 = (f32[256]{0:T(256)}, f32[256]{0:T(256)S(1)}, u32[]{:S(2)}) copy-start(f32[256]{0:T(256)S(1)} %fusion.360) | copy-start | bytes 3076 | tf_op jit(solution)/shard_map/while
  980.0 183.5 %all-gather.35.cloned.1.call-start = ((), (), s32[]{:S(2)}) async-start(), calls=%async_computation.23 | async-start | bytes 1966080 | tf_op jit(solution)/shard_map/while/body/eval_jaxpr/all_gather | solution.py:89
  1035.6 183.7 %all-gather.43.cloned.1.call-start = ((), (), s32[]{:S(2)}) async-start(), calls=%async_computation.27 | async-start | bytes 1216512 | tf_op jit(solution)/shard_map/while/body/eval_jaxpr/all_gather | solution.py:45
  1036.3 248.3 %all-gather.45.cloned.1.call-start = ((), (), s32[]{:S(2)}) async-start(), calls=%async_computation.28 | async-start | bytes 4866048 | tf_op jit(solution)/shard_map/while/body/eval_jaxpr/all_gather | solution.py:49
  1037.0 312.2 %all-gather.47.cloned.1.call-start = ((), (), s32[]{:S(2)}) async-start(), calls=%async_computation.29 | async-start | bytes 4866048 | tf_op jit(solution)/shard_map/while/body/eval_jaxpr/all_gather | solution.py:51
  1037.6 391.2 %reduce-scatter.21.cloned.1.call-start = ((), (), s32[]{:S(2)}) async-start(), calls=%async_computation.30 | async-start | bytes 1966080 | tf_op jit(solution)/shard_map/while/body/eval_jaxpr/reduce_scatter | solution.py:214
  1221.2 141.3 %copy-start.27 = (f32[256]{0:T(256)}, f32[256]{0:T(256)S(1)}, u32[]{:S(2)}) copy-start(f32[256]{0:T(256)S(1)} %broadcast_multiply_fusion.11) | copy-start | bytes 3076 | tf_op jit(solution)/shard_map/while
  1221.4 141.1 %copy-start.32 = (f32[256]{0:T(256)}, f32[256]{0:T(256)S(1)}, u32[]{:S(2)}) copy-start(f32[256]{0:T(256)S(1)} %fusion.366) | copy-start | bytes 3076 | tf_op jit(solution)/shard_map/while
  1221.4 127.8 %copy-start.15 = (bf16[2,256,768]{2,1,0:T(8,128)(2,1)S(1)}, bf16[2,256,768]{2,1,0:T(8,128)(2,1)}, u32[]{:S(2)}) copy-start(bf16[2,256,768]{2,1,0:T(8,128)(2,1)} %get-tuple-element.1195) | copy-start | bytes 2359300 | tf_op jit(solution)/shard_map/while
  1389.1 70.4 %reduce-scatter.23.cloned.1.call-start = ((), (), s32[]{:S(2)}) async-start(), calls=%async_computation.31 | async-start | bytes 1966080 | tf_op jit(solution)/shard_map/while/body/eval_jaxpr/reduce_scatter | solution.py:220
  1467.5 112.1 %copy-start.2 = (bf16[2,256,768]{2,1,0:T(8,128)(2,1)S(1)}, bf16[2,256,768]{2,1,0:T(8,128)(2,1)}, u32[]{:S(2)}) copy-start(bf16[2,256,768]{2,1,0:T(8,128)(2,1)} %get-tuple-element.1180) | copy-start | bytes 2359300 | tf_op jit(solution)/shard_map/while
  1467.5 56.4 %all-gather.39.cloned.1.call-start = ((), (), s32[]{:S(2)}) async-start(), calls=%async_computation.25 | async-start | bytes 1216512 | tf_op jit(solution)/shard_map/while/body/eval_jaxpr/all_gather | solution.py:43
  1468.1 111.6 %all-gather.33.cloned.1.call-start = ((), (), s32[]{:S(2)}) async-start(), calls=%async_computation.22 | async-start | bytes 1216512 | tf_op jit(solution)/shard_map/while/body/eval_jaxpr/all_gather | solution.py:42
  1468.8 166.6 %all-gather.37.cloned.1.call-start = ((), (), s32[]{:S(2)}) async-start(), calls=%async_computation.24 | async-start | bytes 1216512 | tf_op jit(solution)/shard_map/while/body/eval_jaxpr/all_gather | solution.py:40
  1469.6 203.2 %all-gather.41.cloned.1.call-start = ((), (), s32[]{:S(2)}) async-start(), calls=%async_computation.26 | async-start | bytes 1966080 | tf_op jit(solution)/shard_map/while/body/eval_jaxpr/all_gather | solution.py:90
  1517.2 118.2 %copy-start.20 = (f32[256]{0:T(256)}, f32[256]{0:T(256)S(1)}, u32[]{:S(2)}) copy-start(f32[256]{0:T(256)S(1)} %broadcast_multiply_fusion.10) | copy-start | bytes 3076 | tf_op jit(solution)/shard_map/while
  1518.4 117.0 %copy-start.22 = (f32[256]{0:T(256)}, f32[256]{0:T(256)S(1)}, u32[]{:S(2)}) copy-start(f32[256]{0:T(256)S(1)} %fusion.360) | copy-start | bytes 3076 | tf_op jit(solution)/shard_map/while
  1518.5 65.9 %copy-start.65 = (s32[2]{0:T(128)S(1)}, s32[2]{0:T(128)}, u32[]{:S(2)}) copy-start(s32[2]{0:T(128)} %get-tuple-element.1184) | copy-start | bytes 28 | tf_op jit(solution)/shard_map/while
  1526.6 183.7 %all-gather.35.cloned.1.call-start = ((), (), s32[]{:S(2)}) async-start(), calls=%async_computation.23 | async-start | bytes 1966080 | tf_op jit(solution)/shard_map/while/body/eval_jaxpr/all_gather | solution.py:89
  1582.3 183.7 %all-gather.43.cloned.1.call-start = ((), (), s32[]{:S(2)}) async-start(), calls=%async_computation.27 | async-start | bytes 1216512 | tf_op jit(solution)/shard_map/while/body/eval_jaxpr/all_gather | solution.py:45
  1583.0 248.2 %all-gather.45.cloned.1.call-start = ((), (), s32[]{:S(2)}) async-start(), calls=%async_computation.28 | async-start | bytes 4866048 | tf_op jit(solution)/shard_map/while/body/eval_jaxpr/all_gather | solution.py:49
  1583.6 312.3 %all-gather.47.cloned.1.call-start = ((), (), s32[]{:S(2)}) async-start(), calls=%async_computation.29 | async-start | bytes 4866048 | tf_op jit(solution)/shard_map/while/body/eval_jaxpr/all_gather | solution.py:51
  1584.3 398.7 %reduce-scatter.21.cloned.1.call-start = ((), (), s32[]{:S(2)}) async-start(), calls=%async_computation.30 | async-start | bytes 1966080 | tf_op jit(solution)/shard_map/while/body/eval_jaxpr/reduce_scatter | solution.py:214
  1767.9 141.3 %copy-start.27 = (f32[256]{0:T(256)}, f32[256]{0:T(256)S(1)}, u32[]{:S(2)}) copy-start(f32[256]{0:T(256)S(1)} %broadcast_multiply_fusion.11) | copy-start | bytes 3076 | tf_op jit(solution)/shard_map/while
  1768.1 141.1 %copy-start.32 = (f32[256]{0:T(256)}, f32[256]{0:T(256)S(1)}, u32[]{:S(2)}) copy-start(f32[256]{0:T(256)S(1)} %fusion.366) | copy-start | bytes 3076 | tf_op jit(solution)/shard_map/while
  1768.1 127.8 %copy-start.15 = (bf16[2,256,768]{2,1,0:T(8,128)(2,1)S(1)}, bf16[2,256,768]{2,1,0:T(8,128)(2,1)}, u32[]{:S(2)}) copy-start(bf16[2,256,768]{2,1,0:T(8,128)(2,1)} %get-tuple-element.1195) | copy-start | bytes 2359300 | tf_op jit(solution)/shard_map/while
  1935.8 70.4 %reduce-scatter.23.cloned.1.call-start = ((), (), s32[]{:S(2)}) async-start(), calls=%async_computation.31 | async-start | bytes 1966080 | tf_op jit(solution)/shard_map/while/body/eval_jaxpr/reduce_scatter | solution.py:220
  2014.2 104.9 %reduce-scatter.9.cloned.1.call-start = ((), (), s32[]{:S(2)}) async-start(), calls=%async_computation.8 | async-start | bytes 2433024 | tf_op jit(solution)/shard_map/reduce_scatter | solution.py:324
  2014.8 208.7 %reduce-scatter.11.cloned.1.call-start = ((), (), s32[]{:S(2)}) async-start(), calls=%async_computation.9 | async-start | bytes 2433024 | tf_op jit(solution)/shard_map/reduce_scatter | solution.py:324
  2015.4 312.4 %reduce-scatter.13.cloned.1.call-start = ((), (), s32[]{:S(2)}) async-start(), calls=%async_computation.10 | async-start | bytes 2433024 | tf_op jit(solution)/shard_map/reduce_scatter | solution.py:324
  2015.9 416.3 %reduce-scatter.15.cloned.1.call-start = ((), (), s32[]{:S(2)}) async-start(), calls=%async_computation.11 | async-start | bytes 2433024 | tf_op jit(solution)/shard_map/reduce_scatter | solution.py:324
  2016.7 557.3 %reduce-scatter.17.cloned.1.call-start = ((), (), s32[]{:S(2)}) async-start(), calls=%async_computation.12 | async-start | bytes 9732096 | tf_op jit(solution)/shard_map/reduce_scatter | solution.py:324
  2017.4 698.3 %reduce-scatter.19.cloned.1.call-start = ((), (), s32[]{:S(2)}) async-start(), calls=%async_computation.13 | async-start | bytes 9732096 | tf_op jit(solution)/shard_map/reduce_scatter | solution.py:324
  (110 other events, 949.2 us)
Sparse Core Ops, SparseCore 0:
  11.9 56.9 all-gather.22
  71.7 52.8 all-gather.16
  127.4 52.9 all-gather.20
  182.3 35.9 all-gather.24
  220.3 35.8 all-gather.18
  258.9 52.8 all-gather.26
  314.6 62.5 all-gather.28
  379.9 61.8 all-gather.30
  458.4 52.5 all-gather.22
  513.6 52.9 all-gather.16
  569.4 52.9 all-gather.20
  624.4 35.9 all-gather.24
  662.5 35.8 all-gather.18
  701.1 52.8 all-gather.26
  756.6 62.5 all-gather.28
  821.8 61.8 all-gather.30
  924.7 52.6 all-gather.38
  980.0 52.9 all-gather.32
  1035.7 52.8 all-gather.36
  1090.1 35.9 all-gather.40
  1127.7 35.8 all-gather.34
  1166.4 52.8 all-gather.42
  1222.1 62.5 all-gather.44
  1287.3 61.8 all-gather.46
  1389.2 33.7 reduce-scatter.20
  1425.2 34.3 reduce-scatter.22
  1470.8 53.0 all-gather.38
  1526.7 52.8 all-gather.32
  1582.5 52.9 all-gather.36
  1636.8 35.9 all-gather.40
  1674.4 35.8 all-gather.34
  1713.1 52.8 all-gather.42
  1768.7 62.5 all-gather.44
  1834.0 61.8 all-gather.46
  1935.9 33.7 reduce-scatter.20
  1971.9 34.3 reduce-scatter.22
Sparse Core Ops, SparseCore 1:
  2020.5 98.5 reduce-scatter.8
  2124.8 98.6 reduce-scatter.10
  2229.2 98.5 reduce-scatter.12
  2333.7 98.5 reduce-scatter.14
  2438.8 135.2 reduce-scatter.16
  2580.5 135.2 reduce-scatter.18
where the time goes:
time: 2740 us; the launch traced here: 2720 us
  waiting for transfers between devices  2090 us (76%)
  matrix products  274 us (10%)
  blocking collectives  201 us (7%)
  local copies, waits for them, and re-layouts  77.8 us (3%)
  other arithmetic  38.4 us (1%)
    reduce_scatter x6, waiting for transfers between devices, per_device(): lax.psum_scatter(totals, ('dp', 'ctx'), scatter_dimension=0, tiled=True)  652 us
    all_gather x4, waiting for transfers between devices, fetch(): lax.all_gather(shards[11], ('dp', 'ctx'), axis=0, tiled=True)  256 us
    all_gather x4, waiting for transfers between devices, fetch(): lax.all_gather(shards[13], ('dp', 'ctx'), axis=0, tiled=True)  245 us
    all_gather x4, waiting for transfers between devices, fetch(): lax.all_gather(shards[2], ('dp', 'ctx'), axis=0, tiled=True)  195 us
    while x4, blocking collectives  161 us
    all_gather x4, waiting for transfers between devices, fetch(): lax.all_gather(shards[7], ('dp', 'ctx'), axis=0, tiled=True)  155 us
    all_gather x4, waiting for transfers between devices, forward(): lax.all_gather(value_rows, 'ctx', axis=0, tiled=True)  143 us
    all_gather x4, waiting for transfers between devices, forward(): lax.all_gather(key_rows, 'ctx', axis=0, tiled=True)  142 us
  transfers between devices with their start and end apart: 42, of which 40 were waited for; matrix products, arithmetic and copies ran while one was open for 10% of the time, Pallas kernels for 0%

commit v1 on v0

--- a/solution.py
+++ b/solution.py
@@ -54,6 +54,26 @@
 
 
 def forward(tok_block, length, full_set):
+
+    def update_the_quarters(local_x, comm_axis, array_dim):
+        formed, b_next, wide_out = (
+            jax.lax.axis_size(comm_axis),
+            jax.lax.axis_index(comm_axis),
+            local_x.shape[array_dim],
+        )
+        pages = [k0 * formed if j0 == array_dim else k0 for j0, k0 in enumerate(local_x.shape)]
+        near = lax.dynamic_update_slice_in_dim(
+            jnp.zeros(pages, local_x.dtype), local_x, b_next * wide_out, axis=array_dim
+        )
+        for i in range(1, formed):
+            local_x = jax.lax.ppermute(
+                local_x, comm_axis, [(j0, (j0 + 1) % formed) for j0 in range(formed)]
+            )
+            near = lax.dynamic_update_slice_in_dim(
+                near, local_x, (b_next - i) % formed * wide_out, axis=array_dim
+            )
+        return near
+
     (
         ln1_gain,
         ln1_bias,
@@ -87,7 +107,7 @@
     ).astype(jnp.bfloat16)
     all_keys, all_values = (
         lax.all_gather(key_rows, "ctx", axis=0, tiled=True),
-        lax.all_gather(value_rows, "ctx", axis=0, tiled=True),
+        update_the_quarters(value_rows, "ctx", 0),
     )
     total_rows = all_keys.shape[0]
     query_heads = queries.reshape(seq_rows, H, HD)

time: 2740 us -> 2600 us (0.949)
  waiting for transfers between devices: 2090 us -> 1940 us
    all_gather x4 -> x0, waiting for transfers between devices: 143 us -> none  [forward(): lax.all_gather(value_rows, 'ctx', axis=0, tiled=True)]
    all_gather x4, waiting for transfers between devices: 116 us -> 21.4 us  [fetch(): lax.all_gather(shards[4], ('dp', 'ctx'), axis=0, tiled=True)]
    all_gather x4, waiting for transfers between devices: 117 us -> 204 us  [fetch(): lax.all_gather(shards[5], ('dp', 'ctx'), axis=0, tiled=True)]
    ppermute x0 -> x12, waiting for transfers between devices: none -> 86.8 us  [update_the_quarters(): jax.lax.ppermute(local_x, comm_axis, [(j0, (j0 + 1) % formed) for j0 in r...]
    all_gather x4, waiting for transfers between devices: 195 us -> 123 us  [fetch(): lax.all_gather(shards[2], ('dp', 'ctx'), axis=0, tiled=True)]
  transfers between devices with their start and end apart: 42 -> 50, of which waited for: 40 -> 44; matrix products, arithmetic and copies ran while one was open for 10% -> 10% of each run, Pallas kernels for 0% -> 0%
where the time goes in v1:
time: 2600 us; the launch traced here: 2580 us
  waiting for transfers between devices  1940 us (75%)
  matrix products  269 us (10%)
  blocking collectives  201 us (8%)
  local copies, waits for them, and re-layouts  85.9 us (3%)
  other arithmetic  41.9 us (2%)
  loops' own time  27.8 us (1%)
    reduce_scatter x6, waiting for transfers between devices, per_device(): lax.psum_scatter(totals, ('dp', 'ctx'), scatter_dimension=0, tiled=True)  652 us
    all_gather x4, waiting for transfers between devices, fetch(): lax.all_gather(shards[11], ('dp', 'ctx'), axis=0, tiled=True)  256 us
    all_gather x4, waiting for transfers between devices, fetch(): lax.all_gather(shards[13], ('dp', 'ctx'), axis=0, tiled=True)  245 us
    all_gather x4, waiting for transfers between devices, fetch(): lax.all_gather(shards[5], ('dp', 'ctx'), axis=0, tiled=True)  204 us
    while x4, blocking collectives  161 us
    all_gather x4, waiting for transfers between devices, fetch(): lax.all_gather(shards[7], ('dp', 'ctx'), axis=0, tiled=True)  158 us
    all_gather x4, waiting for transfers between devices, forward(): lax.all_gather(key_rows, 'ctx', axis=0, tiled=True)  125 us
    all_gather x4, waiting for transfers between devices, fetch(): lax.all_gather(shards[2], ('dp', 'ctx'), axis=0, tiled=True)  123 us
  transfers between devices with their start and end apart: 50, of which 44 were waited for; matrix products, arithmetic and copies ran while one was open for 10% of the time, Pallas kernels for 0%

profile of v1, /device:TPU:0, one launch (start us, length us, event | category | flops | bytes accessed | tf_op | source)
XLA Modules:
  0.0 2585.0 jit_solution(11883410308774798047)
XLA Ops:
  9.1 820.5 %while.55 = (s32[]{:T(128)}, bf16[2,256,768]{2,1,0:T(8,128)(2,1)}, bf16[2,256,768]{2,1,0:T(8,128)(2,1)}, bf16[24]{0:T(256)(128)(2,1)}, bf16[24]{0:T(256)(128)(2,...) while((s32[]{:T(128)}, bf16[2,256,768]{2,1,0:T(8,128)(2,1)}, ...), condition=%wide.region_7.8_spmd, body=%wide.region_0.7_spmd.sunk | while | flops 4508832256 | bytes 134492976 | solution.py:327
  18.9 42.5 %all-reduce.39 = (bf16[768]{0:T(1024)(128)(2,1)S(1)}, bf16[768]{0:T(1024)(128)(2,1)S(1)}, bf16[768]{0:T(1024)(128)(2,1)S(1)}, bf16[768]{0:T(1024)(128)(2,1)S(1)}...) all-reduce(bf16[768]{0:T(1024)(128)(2,1)S(1)} %dynamic-update-slice, ...), channel_id=1, replica_groups=mesh['dp'=8,'ctx'=4] {'dp','ctx'}, use_global_device_ids=true, to_apply=%add.2 | all-reduce | flops 9216 | bytes 36864 | tf_op jit(solution)/shard_map/while
  74.4 51.0 %all-gather.15.cloned.1.call-done = bf16[768,768]{1,0:T(8,128)(2,1)} async-done(((bf16[24,768]{1,0:T(8,128)(2,1)}), bf16[768,768]{1,0:T(8,128)(2,1)}) %all-gather.15.cloned.1.call-update) | async-done | bytes 1179664 | tf_op jit(solution)/shard_map/while/body/eval_jaxpr/all_gather | solution.py:43
  127.9 12.7 collective-permute-done
  144.1 8.8 collective-permute-done.1
  152.9 34.1 %all-gather.17.cloned.1.call-done = bf16[768,768]{1,0:T(8,128)(2,1)} async-done(((bf16[24,768]{1,0:T(8,128)(2,1)}), bf16[768,768]{1,0:T(8,128)(2,1)}) %all-gather.17.cloned.1.call-update) | async-done | bytes 1179664 | tf_op jit(solution)/shard_map/while/body/eval_jaxpr/all_gather | solution.py:40
  193.1 31.3 %all-gather.21.cloned.1.call-done = bf16[1024,768]{1,0:T(8,128)(2,1)} async-done(((bf16[256,768]{1,0:T(8,128)(2,1)}), bf16[1024,768]{1,0:T(8,128)(2,1)}) %all-gather.21.cloned.1.call-update) | async-done | bytes 1572880 | tf_op jit(solution)/shard_map/while/body/eval_jaxpr/all_gather | solution.py:109
  233.2 7.2 fusion.314
  240.5 39.5 %all-gather.23.cloned.1.call-done = bf16[768,768]{1,0:T(8,128)(2,1)} async-done(((bf16[24,768]{1,0:T(8,128)(2,1)}), bf16[768,768]{1,0:T(8,128)(2,1)}) %all-gather.23.cloned.1.call-update) | async-done | bytes 1179664 | tf_op jit(solution)/shard_map/while/body/eval_jaxpr/all_gather | solution.py:45
  282.1 63.1 %all-gather.25.cloned.1.call-done = bf16[3072,768]{1,0:T(8,128)(2,1)} async-done(((bf16[96,768]{1,0:T(8,128)(2,1)}), bf16[3072,768]{1,0:T(8,128)(2,1)}) %all-gather.25.cloned.1.call-update) | async-done | bytes 4718608 | tf_op jit(solution)/shard_map/while/body/eval_jaxpr/all_gather | solution.py:51
  345.2 64.7 %all-gather.27.cloned.1.call-done = bf16[768,3072]{1,0:T(8,128)(2,1)} async-done(((bf16[24,3072]{1,0:T(8,128)(2,1)}), bf16[768,3072]{1,0:T(8,128)(2,1)}) %all-gather.27.cloned.1.call-update) | async-done | bytes 4718608 | tf_op jit(solution)/shard_map/while/body/eval_jaxpr/all_gather | solution.py:49
  409.9 12.9 fusion.316
  433.4 39.8 %all-reduce.39 = (bf16[768]{0:T(1024)(128)(2,1)S(1)}, bf16[768]{0:T(1024)(128)(2,1)S(1)}, bf16[768]{0:T(1024)(128)(2,1)S(1)}, bf16[768]{0:T(1024)(128)(2,1)S(1)}...) all-reduce(bf16[768]{0:T(1024)(128)(2,1)S(1)} %dynamic-update-slice, ...), channel_id=1, replica_groups=mesh['dp'=8,'ctx'=4] {'dp','ctx'}, use_global_device_ids=true, to_apply=%add.2 | all-reduce | flops 9216 | bytes 36864 | tf_op jit(solution)/shard_map/while
  484.6 51.1 %all-gather.15.cloned.1.call-done = bf16[768,768]{1,0:T(8,128)(2,1)} async-done(((bf16[24,768]{1,0:T(8,128)(2,1)}), bf16[768,768]{1,0:T(8,128)(2,1)}) %all-gather.15.cloned.1.call-update) | async-done | bytes 1179664 | tf_op jit(solution)/shard_map/while/body/eval_jaxpr/all_gather | solution.py:43
  538.2 12.7 collective-permute-done
  554.4 8.8 collective-permute-done.1
  563.2 29.6 %all-gather.17.cloned.1.call-done = bf16[768,768]{1,0:T(8,128)(2,1)} async-done(((bf16[24,768]{1,0:T(8,128)(2,1)}), bf16[768,768]{1,0:T(8,128)(2,1)}) %all-gather.17.cloned.1.call-update) | async-done | bytes 1179664 | tf_op jit(solution)/shard_map/while/body/eval_jaxpr/all_gather | solution.py:40
  598.9 31.4 %all-gather.21.cloned.1.call-done = bf16[1024,768]{1,0:T(8,128)(2,1)} async-done(((bf16[256,768]{1,0:T(8,128)(2,1)}), bf16[1024,768]{1,0:T(8,128)(2,1)}) %all-gather.21.cloned.1.call-update) | async-done | bytes 1572880 | tf_op jit(solution)/shard_map/while/body/eval_jaxpr/all_gather | solution.py:109
  632.1 7.1 fusion.313
  639.2 7.2 fusion.314
  646.4 39.5 %all-gather.23.cloned.1.call-done = bf16[768,768]{1,0:T(8,128)(2,1)} async-done(((bf16[24,768]{1,0:T(8,128)(2,1)}), bf16[768,768]{1,0:T(8,128)(2,1)}) %all-gather.23.cloned.1.call-update) | async-done | bytes 1179664 | tf_op jit(solution)/shard_map/while/body/eval_jaxpr/all_gather | solution.py:45
  688.0 63.2 %all-gather.25.cloned.1.call-done = bf16[3072,768]{1,0:T(8,128)(2,1)} async-done(((bf16[96,768]{1,0:T(8,128)(2,1)}), bf16[3072,768]{1,0:T(8,128)(2,1)}) %all-gather.25.cloned.1.call-update) | async-done | bytes 4718608 | tf_op jit(solution)/shard_map/while/body/eval_jaxpr/all_gather | solution.py:51
  751.2 64.6 %all-gather.27.cloned.1.call-done = bf16[768,3072]{1,0:T(8,128)(2,1)} async-done(((bf16[24,3072]{1,0:T(8,128)(2,1)}), bf16[768,3072]{1,0:T(8,128)(2,1)}) %all-gather.27.cloned.1.call-update) | async-done | bytes 4718608 | tf_op jit(solution)/shard_map/while/body/eval_jaxpr/all_gather | solution.py:49
  815.8 12.9 fusion.316
  830.5 1045.5 %while.56 = (s32[]{:T(128)}, f32[768]{0:T(1024)}, f32[768]{0:T(1024)}, f32[768,768]{1,0:T(8,128)}, f32[768]{0:T(1024)}, /*index=5*/f32[768,768]{1,0:T(8,128)}, f...) while((s32[]{:T(128)}, f32[768]{0:T(1024)}, ...), condition=%wide.region_31.32_spmd.clone, body=%wide.region_8.31_spmd.clone.sunk | while | flops 12278196224 | bytes 527633952 | solution.py:343
  862.0 39.6 %all-reduce.40 = (bf16[768]{0:T(1024)(128)(2,1)S(1)}, bf16[768]{0:T(1024)(128)(2,1)S(1)}, bf16[3072]{0:T(1024)(128)(2,1)S(1)}, bf16[768]{0:T(1024)(128)(2,1)S(1)...) all-reduce(bf16[768]{0:T(1024)(128)(2,1)S(1)} %dynamic-update-slice, ...), channel_id=1, replica_groups=mesh['dp'=8,'ctx'=4] {'dp','ctx'}, use_global_device_ids=true, to_apply=%add.10 | all-reduce | flops 8448 | bytes 33792 | tf_op jit(solution)/shard_map/while
  914.3 50.7 %all-gather.35.cloned.1.call-done = bf16[768,768]{1,0:T(8,128)(2,1)} async-done(((bf16[24,768]{1,0:T(8,128)(2,1)}), bf16[768,768]{1,0:T(8,128)(2,1)}) %all-gather.35.cloned.1.call-update) | async-done | bytes 1179664 | tf_op jit(solution)/shard_map/while/body/eval_jaxpr/all_gather | solution.py:43
  967.5 12.7 collective-permute-done.3
  983.2 9.3 collective-permute-done.4
  992.5 29.6 %all-gather.33.cloned.1.call-done = bf16[768,768]{1,0:T(8,128)(2,1)} async-done(((bf16[24,768]{1,0:T(8,128)(2,1)}), bf16[768,768]{1,0:T(8,128)(2,1)}) %all-gather.33.cloned.1.call-update) | async-done | bytes 1179664 | tf_op jit(solution)/shard_map/while/body/eval_jaxpr/all_gather | solution.py:40
  1028.4 31.1 %all-gather.31.cloned.1.call-done = bf16[1024,768]{1,0:T(8,128)(2,1)} async-done(((bf16[256,768]{1,0:T(8,128)(2,1)}), bf16[1024,768]{1,0:T(8,128)(2,1)}) %all-gather.31.cloned.1.call-update) | async-done | bytes 1572880 | tf_op jit(solution)/shard_map/while/body/eval_jaxpr/all_gather | solution.py:109
  1068.3 7.2 fusion.364
  1075.6 39.7 %all-gather.37.cloned.1.call-done = bf16[768,768]{1,0:T(8,128)(2,1)} async-done(((bf16[24,768]{1,0:T(8,128)(2,1)}), bf16[768,768]{1,0:T(8,128)(2,1)}) %all-gather.37.cloned.1.call-update) | async-done | bytes 1179664 | tf_op jit(solution)/shard_map/while/body/eval_jaxpr/all_gather | solution.py:45
  1117.4 63.1 %all-gather.39.cloned.1.call-done = bf16[768,3072]{1,0:T(8,128)(2,1)} async-done(((bf16[24,3072]{1,0:T(8,128)(2,1)}), bf16[768,3072]{1,0:T(8,128)(2,1)}) %all-gather.39.cloned.1.call-update) | async-done | bytes 4718608 | tf_op jit(solution)/shard_map/while/body/eval_jaxpr/all_gather | solution.py:49
  1186.0 59.2 %all-gather.41.cloned.1.call-done = bf16[3072,768]{1,0:T(8,128)(2,1)} async-done(((bf16[96,768]{1,0:T(8,128)(2,1)}), bf16[3072,768]{1,0:T(8,128)(2,1)}) %all-gather.41.cloned.1.call-update) | async-done | bytes 4718608 | tf_op jit(solution)/shard_map/while/body/eval_jaxpr/all_gather | solution.py:51
  1245.2 11.1 convert_reduce_fusion.15
  1262.8 10.9 multiply_reduce_fusion.12
  1300.3 7.4 fusion.369
  1314.8 10.0 select_add_fusion.38
  1326.8 28.8 %reduce-scatter.23.cloned.1.call-done = bf16[256,768]{0,1:T(8,128)(2,1)} async-done(((bf16[1024,768]{0,1:T(8,128)(2,1)}), bf16[256,768]{0,1:T(8,128)(2,1)}) %reduce-scatter.23.cloned.1.call-update) | async-done | bytes 393232 | tf_op jit(solution)/shard_map/while/body/eval_jaxpr/reduce_scatter | solution.py:240
  1372.1 39.6 %all-reduce.40 = (bf16[768]{0:T(1024)(128)(2,1)S(1)}, bf16[768]{0:T(1024)(128)(2,1)S(1)}, bf16[3072]{0:T(1024)(128)(2,1)S(1)}, bf16[768]{0:T(1024)(128)(2,1)S(1)...) all-reduce(bf16[768]{0:T(1024)(128)(2,1)S(1)} %dynamic-update-slice, ...), channel_id=1, replica_groups=mesh['dp'=8,'ctx'=4] {'dp','ctx'}, use_global_device_ids=true, to_apply=%add.10 | all-reduce | flops 8448 | bytes 33792 | tf_op jit(solution)/shard_map/while
  1424.8 50.8 %all-gather.35.cloned.1.call-done = bf16[768,768]{1,0:T(8,128)(2,1)} async-done(((bf16[24,768]{1,0:T(8,128)(2,1)}), bf16[768,768]{1,0:T(8,128)(2,1)}) %all-gather.35.cloned.1.call-update) | async-done | bytes 1179664 | tf_op jit(solution)/shard_map/while/body/eval_jaxpr/all_gather | solution.py:43
  1478.0 12.7 collective-permute-done.3
  1493.7 9.3 collective-permute-done.4
  1503.0 29.6 %all-gather.33.cloned.1.call-done = bf16[768,768]{1,0:T(8,128)(2,1)} async-done(((bf16[24,768]{1,0:T(8,128)(2,1)}), bf16[768,768]{1,0:T(8,128)(2,1)}) %all-gather.33.cloned.1.call-update) | async-done | bytes 1179664 | tf_op jit(solution)/shard_map/while/body/eval_jaxpr/all_gather | solution.py:40
  1538.9 31.1 %all-gather.31.cloned.1.call-done = bf16[1024,768]{1,0:T(8,128)(2,1)} async-done(((bf16[256,768]{1,0:T(8,128)(2,1)}), bf16[1024,768]{1,0:T(8,128)(2,1)}) %all-gather.31.cloned.1.call-update) | async-done | bytes 1572880 | tf_op jit(solution)/shard_map/while/body/eval_jaxpr/all_gather | solution.py:109
  1571.8 7.1 fusion.362
  1578.8 7.2 fusion.364
  1586.1 39.7 %all-gather.37.cloned.1.call-done = bf16[768,768]{1,0:T(8,128)(2,1)} async-done(((bf16[24,768]{1,0:T(8,128)(2,1)}), bf16[768,768]{1,0:T(8,128)(2,1)}) %all-gather.37.cloned.1.call-update) | async-done | bytes 1179664 | tf_op jit(solution)/shard_map/while/body/eval_jaxpr/all_gather | solution.py:45
  1627.9 63.2 %all-gather.39.cloned.1.call-done = bf16[768,3072]{1,0:T(8,128)(2,1)} async-done(((bf16[24,3072]{1,0:T(8,128)(2,1)}), bf16[768,3072]{1,0:T(8,128)(2,1)}) %all-gather.39.cloned.1.call-update) | async-done | bytes 4718608 | tf_op jit(solution)/shard_map/while/body/eval_jaxpr/all_gather | solution.py:49
  1696.6 59.0 %all-gather.41.cloned.1.call-done = bf16[3072,768]{1,0:T(8,128)(2,1)} async-done(((bf16[96,768]{1,0:T(8,128)(2,1)}), bf16[3072,768]{1,0:T(8,128)(2,1)}) %all-gather.41.cloned.1.call-update) | async-done | bytes 4718608 | tf_op jit(solution)/shard_map/while/body/eval_jaxpr/all_gather | solution.py:51
  1755.7 11.1 convert_reduce_fusion.15
  1773.3 10.9 multiply_reduce_fusion.12
  1804.1 9.4 select_add_fusion.36
  1813.6 7.4 fusion.369
  1830.5 12.2 select_add_fusion.38
  1844.6 21.3 reduce-scatter.23.cloned.1.call-done
  1880.1 40.0 %all-reduce.36 = (f32[768]{0:T(1024)S(1)}, f32[768]{0:T(1024)S(1)}, f32[768]{0:T(1024)S(1)}, f32[768]{0:T(1024)S(1)}, f32[768]{0:T(1024)S(1)}, /*index=5*/f32[76...) all-reduce(f32[768]{0:T(1024)S(1)} %copy-done.64, ...), channel_id=4, replica_groups=mesh['dp'=8,'ctx'=4] {'dp','ctx'}, use_global_device_ids=true, to_apply=%region_32.33.clone | all-reduce | flops 9216 | bytes 73728
  1925.3 55.6 %reduce-scatter.9.cloned.1.call-done = f32[24,768]{1,0:T(8,128)} async-done(((f32[768,768]{1,0:T(8,128)}), f32[24,768]{1,0:T(8,128)}) %reduce-scatter.9.cloned.1.call-update) | async-done | bytes 73744 | tf_op jit(solution)/shard_map/reduce_scatter | solution.py:344
  1980.9 104.4 %reduce-scatter.11.cloned.1.call-done = f32[24,768]{1,0:T(8,128)} async-done(((f32[768,768]{1,0:T(8,128)}), f32[24,768]{1,0:T(8,128)}) %reduce-scatter.11.cloned.1.call-update) | async-done | bytes 73744 | tf_op jit(solution)/shard_map/reduce_scatter | solution.py:344
  2085.3 104.4 %reduce-scatter.13.cloned.1.call-done = f32[24,768]{1,0:T(8,128)} async-done(((f32[768,768]{1,0:T(8,128)}), f32[24,768]{1,0:T(8,128)}) %reduce-scatter.13.cloned.1.call-update) | async-done | bytes 73744 | tf_op jit(solution)/shard_map/reduce_scatter | solution.py:344
  2189.7 104.5 %reduce-scatter.15.cloned.1.call-done = f32[24,768]{1,0:T(8,128)} async-done(((f32[768,768]{1,0:T(8,128)}), f32[24,768]{1,0:T(8,128)}) %reduce-scatter.15.cloned.1.call-update) | async-done | bytes 73744 | tf_op jit(solution)/shard_map/reduce_scatter | solution.py:344
  2294.2 141.7 %reduce-scatter.17.cloned.1.call-done = f32[24,3072]{1,0:T(8,128)} async-done(((f32[768,3072]{1,0:T(8,128)}), f32[24,3072]{1,0:T(8,128)}) %reduce-scatter.17.cloned.1.call-update) | async-done | bytes 294928 | tf_op jit(solution)/shard_map/reduce_scatter | solution.py:344
  2435.9 141.7 %reduce-scatter.19.cloned.1.call-done = f32[96,768]{1,0:T(8,128)} async-done(((f32[3072,768]{1,0:T(8,128)}), f32[96,768]{1,0:T(8,128)}) %reduce-scatter.19.cloned.1.call-update) | async-done | bytes 294928 | tf_op jit(solution)/shard_map/reduce_scatter | solution.py:344
  (689 shorter events, 281.7 us)
Async XLA Ops:
  9.1 60.6 %all-gather.19.cloned.1.call-start = ((), (), s32[]{:S(2)}) async-start(), calls=%async_computation.16 | async-start | bytes 1216512 | tf_op jit(solution)/shard_map/while/body/eval_jaxpr/all_gather | solution.py:42
  9.8 115.6 %all-gather.15.cloned.1.call-start = ((), (), s32[]{:S(2)}) async-start(), calls=%async_computation.14 | async-start | bytes 1216512 | tf_op jit(solution)/shard_map/while/body/eval_jaxpr/all_gather | solution.py:43
  10.6 176.5 %all-gather.17.cloned.1.call-start = ((), (), s32[]{:S(2)}) async-start(), calls=%async_computation.15 | async-start | bytes 1216512 | tf_op jit(solution)/shard_map/while/body/eval_jaxpr/all_gather | solution.py:40
  11.3 213.1 %all-gather.21.cloned.1.call-start = ((), (), s32[]{:S(2)}) async-start(), calls=%async_computation.17 | async-start | bytes 1966080 | tf_op jit(solution)/shard_map/while/body/eval_jaxpr/all_gather | solution.py:109
  72.5 207.5 %all-gather.23.cloned.1.call-start = ((), (), s32[]{:S(2)}) async-start(), calls=%async_computation.18 | async-start | bytes 1216512 | tf_op jit(solution)/shard_map/while/body/eval_jaxpr/all_gather | solution.py:45
  73.1 272.1 %all-gather.25.cloned.1.call-start = ((), (), s32[]{:S(2)}) async-start(), calls=%async_computation.19 | async-start | bytes 4866048 | tf_op jit(solution)/shard_map/while/body/eval_jaxpr/all_gather | solution.py:51
  73.6 336.3 %all-gather.27.cloned.1.call-start = ((), (), s32[]{:S(2)}) async-start(), calls=%async_computation.20 | async-start | bytes 4866048 | tf_op jit(solution)/shard_map/while/body/eval_jaxpr/all_gather | solution.py:49
  127.2 13.3 collective-permute-start
  140.5 12.3 collective-permute-start.1
  152.9 37.8 %collective-permute-start.2 = (bf16[256,768]{1,0:T(8,128)(2,1)S(1)}, bf16[256,768]{1,0:T(8,128)(2,1)}, u32[]{:S(2)}, u32[]{:S(2)}) collective-permute-start(bf16[256,768]{1,0:T(8,128)(2,1)S(1)} %collective-permute-done.1), channel_id=1, source_target_pairs={{0,1},{1,2},{2,3},{3,0},{4,5},{5,6},{6,7},{7,4},{8,9},{9,10},{10,1... | collective-permute-start | bytes 1179656 | tf_op jit(solution)/shard_map/while/body/eval_jaxpr/ppermute | solution.py:69
  240.4 169.5 %copy-start.30 = (bf16[2,256,768]{2,1,0:T(8,128)(2,1)S(1)}, bf16[2,256,768]{2,1,0:T(8,128)(2,1)}, u32[]{:S(2)}) copy-start(bf16[2,256,768]{2,1,0:T(8,128)(2,1)} %get-tuple-element.1430) | copy-start | bytes 2359300 | tf_op jit(solution)/shard_map/while
  240.4 169.5 %copy-start.67 = (f32[768]{0:T(1024)S(1)}, f32[768]{0:T(1024)}, u32[]{:S(2)}) copy-start(f32[768]{0:T(1024)} %convert_element_type.650) | copy-start | bytes 9220 | tf_op jit(solution)/shard_map/while
  240.5 169.5 %copy-start.68 = (f32[768]{0:T(1024)S(1)}, f32[768]{0:T(1024)}, u32[]{:S(2)}) copy-start(f32[768]{0:T(1024)} %convert_element_type.651) | copy-start | bytes 9220 | tf_op jit(solution)/shard_map/while
  240.5 169.5 %copy-start.69 = (f32[768]{0:T(1024)S(1)}, f32[768]{0:T(1024)}, u32[]{:S(2)}) copy-start(f32[768]{0:T(1024)} %convert_element_type.652) | copy-start | bytes 9220 | tf_op jit(solution)/shard_map/while
  423.7 56.2 %all-gather.19.cloned.1.call-start = ((), (), s32[]{:S(2)}) async-start(), calls=%async_computation.16 | async-start | bytes 1216512 | tf_op jit(solution)/shard_map/while/body/eval_jaxpr/all_gather | solution.py:42
  424.4 111.3 %all-gather.15.cloned.1.call-start = ((), (), s32[]{:S(2)}) async-start(), calls=%async_computation.14 | async-start | bytes 1216512 | tf_op jit(solution)/shard_map/while/body/eval_jaxpr/all_gather | solution.py:43
  425.2 167.6 %all-gather.17.cloned.1.call-start = ((), (), s32[]{:S(2)}) async-start(), calls=%async_computation.15 | async-start | bytes 1216512 | tf_op jit(solution)/shard_map/while/body/eval_jaxpr/all_gather | solution.py:40
  425.7 204.6 %all-gather.21.cloned.1.call-start = ((), (), s32[]{:S(2)}) async-start(), calls=%async_computation.17 | async-start | bytes 1966080 | tf_op jit(solution)/shard_map/while/body/eval_jaxpr/all_gather | solution.py:109
  482.7 203.2 %all-gather.23.cloned.1.call-start = ((), (), s32[]{:S(2)}) async-start(), calls=%async_computation.18 | async-start | bytes 1216512 | tf_op jit(solution)/shard_map/while/body/eval_jaxpr/all_gather | solution.py:45
  483.2 268.0 %all-gather.25.cloned.1.call-start = ((), (), s32[]{:S(2)}) async-start(), calls=%async_computation.19 | async-start | bytes 4866048 | tf_op jit(solution)/shard_map/while/body/eval_jaxpr/all_gather | solution.py:51
  484.0 331.8 %all-gather.27.cloned.1.call-start = ((), (), s32[]{:S(2)}) async-start(), calls=%async_computation.20 | async-start | bytes 4866048 | tf_op jit(solution)/shard_map/while/body/eval_jaxpr/all_gather | solution.py:49
  537.5 13.3 collective-permute-start
  550.8 12.3 collective-permute-start.1
  563.2 33.2 %collective-permute-start.2 = (bf16[256,768]{1,0:T(8,128)(2,1)S(1)}, bf16[256,768]{1,0:T(8,128)(2,1)}, u32[]{:S(2)}, u32[]{:S(2)}) collective-permute-start(bf16[256,768]{1,0:T(8,128)(2,1)S(1)} %collective-permute-done.1), channel_id=1, source_target_pairs={{0,1},{1,2},{2,3},{3,0},{4,5},{5,6},{6,7},{7,4},{8,9},{9,10},{10,1... | collective-permute-start | bytes 1179656 | tf_op jit(solution)/shard_map/while/body/eval_jaxpr/ppermute | solution.py:69
  646.3 169.5 %copy-start.30 = (bf16[2,256,768]{2,1,0:T(8,128)(2,1)S(1)}, bf16[2,256,768]{2,1,0:T(8,128)(2,1)}, u32[]{:S(2)}) copy-start(bf16[2,256,768]{2,1,0:T(8,128)(2,1)} %get-tuple-element.1430) | copy-start | bytes 2359300 | tf_op jit(solution)/shard_map/while
  646.4 169.5 %copy-start.67 = (f32[768]{0:T(1024)S(1)}, f32[768]{0:T(1024)}, u32[]{:S(2)}) copy-start(f32[768]{0:T(1024)} %convert_element_type.650) | copy-start | bytes 9220 | tf_op jit(solution)/shard_map/while
  646.4 169.5 %copy-start.68 = (f32[768]{0:T(1024)S(1)}, f32[768]{0:T(1024)}, u32[]{:S(2)}) copy-start(f32[768]{0:T(1024)} %convert_element_type.651) | copy-start | bytes 9220 | tf_op jit(solution)/shard_map/while
  646.4 169.5 %copy-start.69 = (f32[768]{0:T(1024)S(1)}, f32[768]{0:T(1024)}, u32[]{:S(2)}) copy-start(f32[768]{0:T(1024)} %convert_element_type.652) | copy-start | bytes 9220 | tf_op jit(solution)/shard_map/while
  853.4 56.0 %all-gather.29.cloned.1.call-start = ((), (), s32[]{:S(2)}) async-start(), calls=%async_computation.21 | async-start | bytes 1216512 | tf_op jit(solution)/shard_map/while/body/eval_jaxpr/all_gather | solution.py:42
  854.0 111.0 %all-gather.35.cloned.1.call-start = ((), (), s32[]{:S(2)}) async-start(), calls=%async_computation.24 | async-start | bytes 1216512 | tf_op jit(solution)/shard_map/while/body/eval_jaxpr/all_gather | solution.py:43
  854.6 167.5 %all-gather.33.cloned.1.call-start = ((), (), s32[]{:S(2)}) async-start(), calls=%async_computation.23 | async-start | bytes 1216512 | tf_op jit(solution)/shard_map/while/body/eval_jaxpr/all_gather | solution.py:40
  855.2 204.3 %all-gather.31.cloned.1.call-start = ((), (), s32[]{:S(2)}) async-start(), calls=%async_computation.22 | async-start | bytes 1966080 | tf_op jit(solution)/shard_map/while/body/eval_jaxpr/all_gather | solution.py:109
  912.2 203.1 %all-gather.37.cloned.1.call-start = ((), (), s32[]{:S(2)}) async-start(), calls=%async_computation.25 | async-start | bytes 1216512 | tf_op jit(solution)/shard_map/while/body/eval_jaxpr/all_gather | solution.py:45
  912.9 267.5 %all-gather.39.cloned.1.call-start = ((), (), s32[]{:S(2)}) async-start(), calls=%async_computation.26 | async-start | bytes 4866048 | tf_op jit(solution)/shard_map/while/body/eval_jaxpr/all_gather | solution.py:49
  913.5 331.7 %all-gather.41.cloned.1.call-start = ((), (), s32[]{:S(2)}) async-start(), calls=%async_computation.27 | async-start | bytes 4866048 | tf_op jit(solution)/shard_map/while/body/eval_jaxpr/all_gather | solution.py:51
  914.3 410.5 %reduce-scatter.21.cloned.1.call-start = ((), (), s32[]{:S(2)}) async-start(), calls=%async_computation.28 | async-start | bytes 1966080 | tf_op jit(solution)/shard_map/while/body/eval_jaxpr/reduce_scatter | solution.py:234
  966.9 13.3 collective-permute-start.3
  980.2 12.3 collective-permute-start.4
  992.5 33.5 %collective-permute-start.5 = (bf16[256,768]{1,0:T(8,128)(2,1)S(1)}, bf16[256,768]{1,0:T(8,128)(2,1)}, u32[]{:S(2)}, u32[]{:S(2)}) collective-permute-start(bf16[256,768]{1,0:T(8,128)(2,1)S(1)} %collective-permute-done.4), channel_id=1, source_target_pairs={{0,1},{1,2},{2,3},{3,0},{4,5},{5,6},{6,7},{7,4},{8,9},{9,10},{10,1... | collective-permute-start | bytes 1179656 | tf_op jit(solution)/shard_map/while/body/eval_jaxpr/ppermute | solution.py:69
  1117.1 141.3 %copy-start.32 = (f32[256]{0:T(256)}, f32[256]{0:T(256)S(1)}, u32[]{:S(2)}) copy-start(f32[256]{0:T(256)S(1)} %broadcast_multiply_fusion.11) | copy-start | bytes 3076 | tf_op jit(solution)/shard_map/while
  1117.4 141.1 %copy-start.37 = (f32[256]{0:T(256)}, f32[256]{0:T(256)S(1)}, u32[]{:S(2)}) copy-start(f32[256]{0:T(256)S(1)} %fusion.366) | copy-start | bytes 3076 | tf_op jit(solution)/shard_map/while
  1117.4 127.8 %copy-start.17 = (bf16[2,256,768]{2,1,0:T(8,128)(2,1)S(1)}, bf16[2,256,768]{2,1,0:T(8,128)(2,1)}, u32[]{:S(2)}) copy-start(bf16[2,256,768]{2,1,0:T(8,128)(2,1)} %get-tuple-element.1623) | copy-start | bytes 2359300 | tf_op jit(solution)/shard_map/while
  1284.9 70.6 %reduce-scatter.23.cloned.1.call-start = ((), (), s32[]{:S(2)}) async-start(), calls=%async_computation.29 | async-start | bytes 1966080 | tf_op jit(solution)/shard_map/while/body/eval_jaxpr/reduce_scatter | solution.py:240
  1363.4 56.4 %all-gather.29.cloned.1.call-start = ((), (), s32[]{:S(2)}) async-start(), calls=%async_computation.21 | async-start | bytes 1216512 | tf_op jit(solution)/shard_map/while/body/eval_jaxpr/all_gather | solution.py:42
  1364.0 111.6 %all-gather.35.cloned.1.call-start = ((), (), s32[]{:S(2)}) async-start(), calls=%async_computation.24 | async-start | bytes 1216512 | tf_op jit(solution)/shard_map/while/body/eval_jaxpr/all_gather | solution.py:43
  1364.7 167.9 %all-gather.33.cloned.1.call-start = ((), (), s32[]{:S(2)}) async-start(), calls=%async_computation.23 | async-start | bytes 1216512 | tf_op jit(solution)/shard_map/while/body/eval_jaxpr/all_gather | solution.py:40
  1365.3 204.7 %all-gather.31.cloned.1.call-start = ((), (), s32[]{:S(2)}) async-start(), calls=%async_computation.22 | async-start | bytes 1966080 | tf_op jit(solution)/shard_map/while/body/eval_jaxpr/all_gather | solution.py:109
  1422.6 203.1 %all-gather.37.cloned.1.call-start = ((), (), s32[]{:S(2)}) async-start(), calls=%async_computation.25 | async-start | bytes 1216512 | tf_op jit(solution)/shard_map/while/body/eval_jaxpr/all_gather | solution.py:45
  1423.4 267.7 %all-gather.39.cloned.1.call-start = ((), (), s32[]{:S(2)}) async-start(), calls=%async_computation.26 | async-start | bytes 4866048 | tf_op jit(solution)/shard_map/while/body/eval_jaxpr/all_gather | solution.py:49
  1424.1 331.6 %all-gather.41.cloned.1.call-start = ((), (), s32[]{:S(2)}) async-start(), calls=%async_computation.27 | async-start | bytes 4866048 | tf_op jit(solution)/shard_map/while/body/eval_jaxpr/all_gather | solution.py:51
  1424.7 418.0 %reduce-scatter.21.cloned.1.call-start = ((), (), s32[]{:S(2)}) async-start(), calls=%async_computation.28 | async-start | bytes 1966080 | tf_op jit(solution)/shard_map/while/body/eval_jaxpr/reduce_scatter | solution.py:234
  1477.4 13.3 collective-permute-start.3
  1490.7 12.3 collective-permute-start.4
  1503.0 33.5 %collective-permute-start.5 = (bf16[256,768]{1,0:T(8,128)(2,1)S(1)}, bf16[256,768]{1,0:T(8,128)(2,1)}, u32[]{:S(2)}, u32[]{:S(2)}) collective-permute-start(bf16[256,768]{1,0:T(8,128)(2,1)S(1)} %collective-permute-done.4), channel_id=1, source_target_pairs={{0,1},{1,2},{2,3},{3,0},{4,5},{5,6},{6,7},{7,4},{8,9},{9,10},{10,1... | collective-permute-start | bytes 1179656 | tf_op jit(solution)/shard_map/while/body/eval_jaxpr/ppermute | solution.py:69
  1627.6 141.3 %copy-start.32 = (f32[256]{0:T(256)}, f32[256]{0:T(256)S(1)}, u32[]{:S(2)}) copy-start(f32[256]{0:T(256)S(1)} %broadcast_multiply_fusion.11) | copy-start | bytes 3076 | tf_op jit(solution)/shard_map/while
  1627.8 141.1 %copy-start.37 = (f32[256]{0:T(256)}, f32[256]{0:T(256)S(1)}, u32[]{:S(2)}) copy-start(f32[256]{0:T(256)S(1)} %fusion.366) | copy-start | bytes 3076 | tf_op jit(solution)/shard_map/while
  1627.8 127.8 %copy-start.17 = (bf16[2,256,768]{2,1,0:T(8,128)(2,1)S(1)}, bf16[2,256,768]{2,1,0:T(8,128)(2,1)}, u32[]{:S(2)}) copy-start(bf16[2,256,768]{2,1,0:T(8,128)(2,1)} %get-tuple-element.1623) | copy-start | bytes 2359300 | tf_op jit(solution)/shard_map/while
  1795.4 70.6 %reduce-scatter.23.cloned.1.call-start = ((), (), s32[]{:S(2)}) async-start(), calls=%async_computation.29 | async-start | bytes 1966080 | tf_op jit(solution)/shard_map/while/body/eval_jaxpr/reduce_scatter | solution.py:240
  1876.0 104.9 %reduce-scatter.9.cloned.1.call-start = ((), (), s32[]{:S(2)}) async-start(), calls=%async_computation.8 | async-start | bytes 2433024 | tf_op jit(solution)/shard_map/reduce_scatter | solution.py:344
  1876.6 208.7 %reduce-scatter.11.cloned.1.call-start = ((), (), s32[]{:S(2)}) async-start(), calls=%async_computation.9 | async-start | bytes 2433024 | tf_op jit(solution)/shard_map/reduce_scatter | solution.py:344
  1877.2 312.5 %reduce-scatter.13.cloned.1.call-start = ((), (), s32[]{:S(2)}) async-start(), calls=%async_computation.10 | async-start | bytes 2433024 | tf_op jit(solution)/shard_map/reduce_scatter | solution.py:344
  1877.8 416.5 %reduce-scatter.15.cloned.1.call-start = ((), (), s32[]{:S(2)}) async-start(), calls=%async_computation.11 | async-start | bytes 2433024 | tf_op jit(solution)/shard_map/reduce_scatter | solution.py:344
  1878.5 557.4 %reduce-scatter.17.cloned.1.call-start = ((), (), s32[]{:S(2)}) async-start(), calls=%async_computation.12 | async-start | bytes 9732096 | tf_op jit(solution)/shard_map/reduce_scatter | solution.py:344
  1879.2 698.4 %reduce-scatter.19.cloned.1.call-start = ((), (), s32[]{:S(2)}) async-start(), calls=%async_computation.13 | async-start | bytes 9732096 | tf_op jit(solution)/shard_map/reduce_scatter | solution.py:344
  (137 other events, 2662.4 us)
Sparse Core Ops, SparseCore 0:
  12.7 56.9 all-gather.18
  72.5 52.8 all-gather.14
  128.2 58.7 all-gather.16
  188.4 35.9 all-gather.20
  227.1 52.8 all-gather.22
  282.6 62.5 all-gather.24
  348.0 61.8 all-gather.26
  427.3 52.5 all-gather.18
  482.7 52.9 all-gather.14
  538.4 54.3 all-gather.16
  594.4 35.9 all-gather.20
  633.0 52.8 all-gather.22
  688.7 62.5 all-gather.24
  753.9 61.8 all-gather.26
  856.8 52.6 all-gather.28
  912.1 52.9 all-gather.34
  967.7 54.3 all-gather.32
  1023.5 35.9 all-gather.30
  1062.3 52.8 all-gather.36
  1117.9 62.5 all-gather.38
  1183.3 61.8 all-gather.40
  1285.0 33.7 reduce-scatter.20
  1321.1 34.3 reduce-scatter.22
  1366.7 53.0 all-gather.28
  1422.6 52.8 all-gather.34
  1478.2 54.3 all-gather.32
  1534.0 35.9 all-gather.30
  1572.8 52.8 all-gather.36
  1628.5 62.5 all-gather.38
  1693.7 61.8 all-gather.40
  1795.5 33.7 reduce-scatter.20
  1831.6 34.2 reduce-scatter.22
Sparse Core Ops, SparseCore 1:
  1882.3 98.5 reduce-scatter.8
  1986.7 98.6 reduce-scatter.10
  2091.0 98.6 reduce-scatter.12
  2195.6 98.6 reduce-scatter.14
  2300.7 135.1 reduce-scatter.16
  2442.4 135.2 reduce-scatter.18
